TPU v7x, 256 devices: a whole 4x4x8 slice. The times are simulated.
256 devices in a mesh: gx: 16 (over z, core), gy: 16 (over x, y).
Axes of the slice: x: 4, y: 4, z: 8, core: 2. Of those that a mesh axis runs over, the one named last changes fastest.
Arguments:
- state: bfloat16 [2, 256, 768, 2048], P(None, None, 'gx', 'gy'), as said below
Outputs:
- modes: bfloat16 [255, 2, 768, 2048], P(None, None, 'gx', 'gy')
- reduced: float32 [255, 255], replicated
Inputs may be any that keep to these rules, and one draw needn't show every extreme that they name: `state`: both fields are positive.
All inputs are finite; a program needn't handle non-finite values.
Results may differ from a plain program's by a relative error of at most 0.0077.
Values may be sent and summed in bfloat16 or wider, within the bound.
No kernel may reach another device: no remote copies, remote signals or barrier semaphores. Data moves between devices by JAX's collectives and lax.ppermute only.
A program may use at most 128 MiB of HBM per device.

v0:
```python
import jax
import jax.numpy as jnp
from jax import lax
from jax.experimental import pallas as pl
from jax.experimental.pallas import tpu as pltpu
from jax.sharding import PartitionSpec as P

BLOCK = 32


def feature_kernel(dens_ref, ener_ref, xh_ref, yh_ref, out_ref):
    nx = dens_ref.shape[2]
    ny = dens_ref.shape[3]
    lanes = yh_ref.shape[2]
    rows = lax.broadcasted_iota(jnp.int32, (nx, ny), 0)
    cols = lax.broadcasted_iota(jnp.int32, (nx, ny), 1)

    def body(s, carry):
        temp = 0.4 * ener_ref[0, s].astype(jnp.float32) / dens_ref[0, s].astype(jnp.float32)
        xh = xh_ref[s]
        halo = pltpu.roll(yh_ref[0], (ny - 2 - 4 * s) % lanes, 1)
        up2 = jnp.where(rows == 0, xh[0:1], jnp.where(rows == 1, xh[1:2], pltpu.roll(temp, 2, 0)))
        up1 = jnp.where(rows == 0, xh[1:2], pltpu.roll(temp, 1, 0))
        dn1 = jnp.where(rows == nx - 1, xh[2:3], pltpu.roll(temp, nx - 1, 0))
        dn2 = jnp.where(rows == nx - 2, xh[2:3], jnp.where(rows == nx - 1, xh[3:4], pltpu.roll(temp, nx - 2, 0)))
        lf2 = pltpu.roll(jnp.where(cols >= ny - 2, halo, temp), 2, 1)
        lf1 = pltpu.roll(jnp.where(cols == ny - 1, halo, temp), 1, 1)
        rt1 = pltpu.roll(jnp.where(cols == 0, halo, temp), ny - 1, 1)
        rt2 = pltpu.roll(jnp.where(cols < 2, halo, temp), ny - 2, 1)
        grad_x = (up2 - 8.0 * up1 + 8.0 * dn1 - dn2) / 12.0
        grad_y = (lf2 - 8.0 * lf1 + 8.0 * rt1 - rt2) / 12.0
        out_ref[s, 0] = grad_x.astype(out_ref.dtype)
        out_ref[s, 1] = grad_y.astype(out_ref.dtype)
        return carry

    lax.fori_loop(0, dens_ref.shape[1], body, 0, unroll=8)


def features_of(state, xh, yh):
    _, snaps, nx, ny = state.shape
    block = min(BLOCK, snaps)
    lanes = yh.shape[-1]
    return pl.pallas_call(
        feature_kernel,
        grid=(snaps // block,),
        in_specs=[
            pl.BlockSpec((1, block, nx, ny), lambda i: (0, i, 0, 0)),
            pl.BlockSpec((1, block, nx, ny), lambda i: (1, i, 0, 0)),
            pl.BlockSpec((block, 4, ny), lambda i: (i, 0, 0)),
            pl.BlockSpec((1, nx, lanes), lambda i: (i, 0, 0)),
        ],
        out_specs=pl.BlockSpec((block, 2, nx, ny), lambda i: (i, 0, 0, 0)),
        out_shape=jax.ShapeDtypeStruct((snaps, 2, nx, ny), jnp.bfloat16),
    )(state, state, xh, yh)


def edge_kernel(dens_ref, ener_ref, out_ref):
    nx = dens_ref.shape[2]
    ny = dens_ref.shape[3]
    group = lax.broadcasted_iota(jnp.int32, (nx, ny), 1) // 4

    def body(s, slab):
        temp = 0.4 * ener_ref[0, s].astype(jnp.float32) / dens_ref[0, s].astype(jnp.float32)
        return jnp.where(group == s, pltpu.roll(temp, (4 * s + 2) % ny, 1), slab)

    out_ref[0] = lax.fori_loop(0, dens_ref.shape[1], body, jnp.zeros((nx, ny), jnp.float32), unroll=8)


def edges_of(state):
    _, snaps, nx, ny = state.shape
    block = ny // 4
    return pl.pallas_call(
        edge_kernel,
        grid=(snaps // block,),
        in_specs=[
            pl.BlockSpec((1, block, nx, ny), lambda i: (0, i, 0, 0)),
            pl.BlockSpec((1, block, nx, ny), lambda i: (1, i, 0, 0)),
        ],
        out_specs=pl.BlockSpec((1, nx, ny), lambda i: (i, 0, 0)),
        out_shape=jax.ShapeDtypeStruct((snaps // block, nx, ny), jnp.float32),
    )(state, state)


def pack_symmetric(gram):
    half = gram.shape[0] // 2
    upper_left = gram[:half, :half]
    lower_right = gram[half:, half:]
    rows = lax.broadcasted_iota(jnp.int32, (half, half), 0)
    cols = lax.broadcasted_iota(jnp.int32, (half, half), 1)
    folded = jnp.where(rows >= cols, upper_left, lower_right)
    return jnp.concatenate(
        [gram[half:, :half], folded, jnp.diagonal(lower_right)[None]], axis=0
    )


def unpack_symmetric(packed):
    half = packed.shape[1]
    block = packed[:half]
    folded = packed[half : 2 * half]
    diag = packed[2 * half]
    rows = lax.broadcasted_iota(jnp.int32, (half, half), 0)
    cols = lax.broadcasted_iota(jnp.int32, (half, half), 1)
    upper_left = jnp.where(rows >= cols, folded, folded.T)
    lower_right = jnp.where(rows < cols, folded, folded.T)
    lower_right = jnp.where(rows == cols, diag[None, :], lower_right)
    return jnp.concatenate(
        [
            jnp.concatenate([upper_left, block.T], axis=1),
            jnp.concatenate([block, lower_right], axis=1),
        ],
        axis=0,
    )


def doubling_sum(value, axis):
    count = lax.axis_size(axis)
    step = 1
    while step < count:
        value = value + lax.ppermute(value, axis, [(i, i ^ step) for i in range(count)])
        step *= 2
    return value


def tri_solve(lower, right):
    return lax.linalg.triangular_solve(lower, right, left_side=True, lower=True)


def shards(state):
    snaps = state.shape[1]
    rows_x = state.shape[2]
    rows_y = state.shape[3]
    total_rows = 2 * rows_x * rows_y * lax.axis_size("gx") * lax.axis_size("gy")
    def temp_of(region):
        return 0.4 * state[(1,) + region].astype(jnp.float32) / state[(0,) + region].astype(jnp.float32)

    def shifted_pair(first, last, axis):
        count = lax.axis_size(axis)
        down = lax.ppermute(last, axis, [(i, i + 1) for i in range(count - 1)])
        up = lax.ppermute(first, axis, [(i + 1, i) for i in range(count - 1)])
        return down, up

    every = slice(None)
    top, bottom = shifted_pair(
        temp_of((every, slice(0, 2))), temp_of((every, slice(rows_x - 2, rows_x))), "gx"
    )
    slab = edges_of(state)
    count = lax.axis_size("gy")
    from_left = lax.ppermute(slab, "gy", [(i, i + 1) for i in range(count - 1)])
    from_right = lax.ppermute(slab, "gy", [(i + 1, i) for i in range(count - 1)])
    lane = lax.broadcasted_iota(jnp.int32, slab.shape, 2)
    features = features_of(
        state,
        jnp.concatenate([top, bottom], axis=1),
        jnp.where(lane % 4 < 2, from_left, from_right),
    )
    local_gram = (
        lax.dot_general(
            features, features, (((1, 2, 3), (1, 2, 3)), ((), ())), preferred_element_type=jnp.float32
        )
        / total_rows
    )
    packed = doubling_sum(doubling_sum(pack_symmetric(local_gram), "gx"), "gy")
    gram = unpack_symmetric(packed)
    lower = jnp.linalg.cholesky(gram[: snaps - 1, : snaps - 1])
    cross = gram[: snaps - 1, 1:]
    inverse = tri_solve(lower, jnp.eye(snaps - 1, dtype=jnp.float32))
    highest = lax.Precision.HIGHEST
    reduced = jnp.dot(jnp.dot(inverse, cross, precision=highest), inverse.T, precision=highest)
    shifted = jnp.concatenate(
        [jnp.zeros((snaps - 1, 1), jnp.bfloat16), inverse.astype(jnp.bfloat16)], axis=1
    )
    modes = lax.dot_general(
        shifted, features, (((1,), (0,)), ((), ())), preferred_element_type=jnp.float32
    ).astype(jnp.bfloat16)
    return (modes, reduced)


def solution(mesh):
    placed = (P(None, None, "gx", "gy"),)
    return jax.shard_map(
        shards,
        mesh=mesh,
        in_specs=placed,
        out_specs=(P(None, None, "gx", "gy"), P()),
        check_vma=False,
    )
```

profile of v0, /device:TPU:24, one launch (start us, length us, event | category | flops | bytes accessed | tf_op | source)
XLA Modules:
  0.0 188.7 jit_solution(17527735514219987199)
XLA Ops:
  0.6 7.9 %shard_map.30 = f32[8,48,128]{2,1,0:T(8,128)} custom-call(bf16[2,256,48,128]{3,2,1,0:T(8,128)(2,1)} %ener_ref.3, bf16[2,256,48,128]{3,2,1,0:T(8,128)(2,1)} %ener_ref.3), custom_call_target="tpu_custom_call" | custom-call | tf_op jit(solution)/shard_map/pallas_call | solution.py:72
  8.6 2.6 %collective-permute-start.3 = (f32[8,48,128]{2,1,0:T(8,128)}, f32[8,48,128]{2,1,0:T(8,128)S(1)}, u32[]{:S(2)}, u32[]{:S(2)}) collective-permute-start(f32[8,48,128]{2,1,0:T(8,128)} %shard_map.30), channel_id=1, source_target_pairs={{1,0},{2,1},{3,2},{4,3},{5,4},{6,5},{7,6},{8,7},{9,8},{10,9},{11,1... | collective-permute-start | bytes 589832 | tf_op jit(solution)/shard_map/ppermute | solution.py:149
  11.2 5.3 %collective-permute-start.2 = (f32[8,48,128]{2,1,0:T(8,128)}, f32[8,48,128]{2,1,0:T(8,128)S(1)}, u32[]{:S(2)}, u32[]{:S(2)}) collective-permute-start(f32[8,48,128]{2,1,0:T(8,128)} %shard_map.30), channel_id=1, source_target_pairs={{0,1},{1,2},{2,3},{3,4},{4,5},{5,6},{6,7},{7,8},{8,9},{9,10},{10,1... | collective-permute-start | bytes 589832 | tf_op jit(solution)/shard_map/ppermute | solution.py:148
  16.5 2.0 %fusion.17 = (f32[256,2,128]{2,1,0:T(2,128)S(1)}, f32[256,2,128]{2,1,0:T(2,128)S(1)}) fusion(bf16[2,256,48,128]{3,2,1,0:T(8,128)(2,1)} %ener_ref.3), kind=kLoop, calls=%fused_computation.22 | loop fusion | flops 524288 | bytes 1048576 | tf_op jit(solution)/shard_map/div | solution.py:134
  18.6 1.3 collective-permute-start
  19.9 1.3 collective-permute-start.1
  21.2 0.7 fusion.18.yh_ref
  21.9 3.5 %collective-permute-done.1 = f32[256,2,128]{2,1,0:T(2,128)S(1)} collective-permute-done((f32[256,2,128]{2,1,0:T(2,128)S(1)}, f32[256,2,128]{2,1,0:T(2,128)S(1)}, u32[]{:S(2)}, u32[]{:S(2)}) %collective-permute-start.1) | collective-permute-done | bytes 262176 | tf_op jit(solution)/shard_map/ppermute | solution.py:139
  25.4 1.0 pad_maximum_fusion.xh_ref
  26.5 21.6 %shard_map.31 = bf16[256,2,48,128]{3,2,1,0:T(8,128)(2,1)} custom-call(bf16[2,256,48,128]{3,2,1,0:T(8,128)(2,1)} %ener_ref.3, bf16[2,256,48,128]{3,2,1,0:T(8,128)(2,1)} %ener_ref.3, f32[256,4,128]{2,1,0:T(4,128)} %pad_maximum_fusion.xh_ref, f32[8,48,128]{2,1,0:T(8,128)} %fusion.18.yh_ref), custom_call_target="tpu_custom_call" | custom-call | tf_op jit(solution)/shard_map/pallas_call | solution.py:43
  48.1 8.0 %fusion.10 = f32[256,256]{1,0:T(8,128)S(1)} fusion(bf16[256,2,48,128]{3,2,1,0:T(8,128)(2,1)} %shard_map.31), kind=kOutput, calls=%fused_computation.7 | convolution fusion | flops 1610678272 | bytes 6553600 | tf_op jit(solution)/shard_map/dot_general | solution.py:157
  56.1 1.2 gather_fusion
  57.4 4.8 %collective-permute-start.4 = (f32[257,128]{1,0:T(8,128)S(1)}, f32[257,128]{1,0:T(8,128)S(1)}, u32[]{:S(2)}, u32[]{:S(2)}) collective-permute-start(f32[257,128]{1,0:T(8,128)S(1)} %pad_maximum_fusion.4), channel_id=1, source_target_pairs={{0,16},{16,0},{32,48},{48,32},{64,80},{80,64},{96,112},{112,96},{1... | collective-permute-start | bytes 394760 | tf_op jit(solution)/shard_map/ppermute | solution.py:119
  62.2 1.0 collective-permute-done.4
  63.2 2.0 %collective-permute-start.5 = (f32[257,128]{1,0:T(8,128)S(1)}, f32[257,128]{1,0:T(8,128)S(1)}, u32[]{:S(2)}, u32[]{:S(2)}) collective-permute-start(f32[257,128]{1,0:T(8,128)S(1)} %fusion.35), channel_id=1, source_target_pairs={{0,32},{16,48},{32,0},{48,16},{64,96},{80,112},{96,64},{112,80},{1... | collective-permute-start | bytes 394760 | tf_op jit(solution)/shard_map/ppermute | solution.py:119
  65.3 4.1 %collective-permute-done.5 = f32[257,128]{1,0:T(8,128)S(1)} collective-permute-done((f32[257,128]{1,0:T(8,128)S(1)}, f32[257,128]{1,0:T(8,128)S(1)}, u32[]{:S(2)}, u32[]{:S(2)}) %collective-permute-start.5) | collective-permute-done | bytes 131616 | tf_op jit(solution)/shard_map/ppermute | solution.py:119
  69.4 5.8 %collective-permute-start.6 = (f32[257,128]{1,0:T(8,128)S(1)}, f32[257,128]{1,0:T(8,128)S(1)}, u32[]{:S(2)}, u32[]{:S(2)}) collective-permute-start(f32[257,128]{1,0:T(8,128)S(1)} %add.63), channel_id=1, source_target_pairs={{0,64},{16,80},{32,96},{48,112},{64,0},{80,16},{96,32},{112,48},{1... | collective-permute-start | bytes 394760 | tf_op jit(solution)/shard_map/ppermute | solution.py:119
  75.2 6.4 %collective-permute-done.6 = f32[257,128]{1,0:T(8,128)S(1)} collective-permute-done((f32[257,128]{1,0:T(8,128)S(1)}, f32[257,128]{1,0:T(8,128)S(1)}, u32[]{:S(2)}, u32[]{:S(2)}) %collective-permute-start.6) | collective-permute-done | bytes 131616 | tf_op jit(solution)/shard_map/ppermute | solution.py:119
  81.6 2.7 %collective-permute-start.7 = (f32[257,128]{1,0:T(8,128)S(1)}, f32[257,128]{1,0:T(8,128)S(1)}, u32[]{:S(2)}, u32[]{:S(2)}) collective-permute-start(f32[257,128]{1,0:T(8,128)S(1)} %add.64), channel_id=1, source_target_pairs={{0,128},{16,144},{32,160},{48,176},{64,192},{80,208},{96,224},{112... | collective-permute-start | bytes 394760 | tf_op jit(solution)/shard_map/ppermute | solution.py:119
  84.4 8.2 %collective-permute-done.7 = f32[257,128]{1,0:T(8,128)S(1)} collective-permute-done((f32[257,128]{1,0:T(8,128)S(1)}, f32[257,128]{1,0:T(8,128)S(1)}, u32[]{:S(2)}, u32[]{:S(2)}) %collective-permute-start.7) | collective-permute-done | bytes 131616 | tf_op jit(solution)/shard_map/ppermute | solution.py:119
  92.6 0.1 collective-permute-start.8
  92.7 5.4 %collective-permute-done.8 = f32[257,128]{1,0:T(8,128)S(1)} collective-permute-done((f32[257,128]{1,0:T(8,128)S(1)}, f32[257,128]{1,0:T(8,128)S(1)}, u32[]{:S(2)}, u32[]{:S(2)}) %collective-permute-start.8) | collective-permute-done | bytes 131616 | tf_op jit(solution)/shard_map/ppermute | solution.py:119
  98.1 0.1 collective-permute-start.9
  98.2 6.5 %collective-permute-done.9 = f32[257,128]{1,0:T(8,128)S(1)} collective-permute-done((f32[257,128]{1,0:T(8,128)S(1)}, f32[257,128]{1,0:T(8,128)S(1)}, u32[]{:S(2)}, u32[]{:S(2)}) %collective-permute-start.9) | collective-permute-done | bytes 131616 | tf_op jit(solution)/shard_map/ppermute | solution.py:119
  104.8 1.6 collective-permute-start.10
  106.4 3.5 %collective-permute-done.10 = f32[257,128]{1,0:T(8,128)S(1)} collective-permute-done((f32[257,128]{1,0:T(8,128)S(1)}, f32[257,128]{1,0:T(8,128)S(1)}, u32[]{:S(2)}, u32[]{:S(2)}) %collective-permute-start.10) | collective-permute-done | bytes 131616 | tf_op jit(solution)/shard_map/ppermute | solution.py:119
  109.9 3.3 %collective-permute-start.11 = (f32[257,128]{1,0:T(8,128)S(1)}, f32[257,128]{1,0:T(8,128)S(1)}, u32[]{:S(2)}, u32[]{:S(2)}) collective-permute-start(f32[257,128]{1,0:T(8,128)S(1)} %add.68), channel_id=1, source_target_pairs={{0,8},{1,9},{2,10},{3,11},{4,12},{5,13},{6,14},{7,15},{8,0},{9,1},... | collective-permute-start | bytes 394760 | tf_op jit(solution)/shard_map/ppermute | solution.py:119
  113.2 0.1 copy.18
  113.3 0.1 copy.15
  113.5 3.2 %collective-permute-done.11 = f32[257,128]{1,0:T(8,128)S(1)} collective-permute-done((f32[257,128]{1,0:T(8,128)S(1)}, f32[257,128]{1,0:T(8,128)S(1)}, u32[]{:S(2)}, u32[]{:S(2)}) %collective-permute-start.11) | collective-permute-done | bytes 131616 | tf_op jit(solution)/shard_map/ppermute | solution.py:119
  116.7 0.1 copy.19
  116.8 0.1 copy.16
  117.0 0.1 copy.20
  117.2 11.7 %cholesky.57 = f32[128,128]{1,0:T(8,128)S(1)} custom-call(f32[128,128]{1,0:T(8,128)S(1)} %cholesky.131), custom_call_target="Cholesky" | custom-call | tf_op jit(solution)/shard_map/jit(cholesky)/cholesky | solution.py:164
  129.0 0.6 compare_reduce_fusion.1
  129.6 9.8 %custom-call.14 = f32[1,128,128]{1,2,0:T(8,128)S(1)} custom-call(f32[1,128,128]{2,1,0:T(8,128)S(1)} %get-tuple-element.39), custom_call_target="InvertDiagBlocksLowerTriangular" | custom-call | tf_op jit(solution)/shard_map/jit(cholesky)/cholesky | solution.py:164
  139.5 0.2 constant_dynamic-update-slice_fusion.1
  139.7 0.3 convolution_subtract_fusion.1
  139.9 11.6 %cholesky.117 = f32[127,127]{1,0:T(8,128)S(1)} custom-call(f32[127,127]{1,0:T(8,128)S(1)} %convolution_subtract_fusion.1), custom_call_target="Cholesky" | custom-call | tf_op jit(solution)/shard_map/jit(cholesky)/cholesky | solution.py:164
  151.6 0.6 compare_reduce_fusion
  153.7 19.9 %custom-call.15 = f32[2,128,128]{1,2,0:T(8,128)S(1)} custom-call(f32[2,128,128]{2,1,0:T(8,128)S(1)} %pad_maximum_fusion.5), custom_call_target="InvertDiagBlocksLowerTriangular" | custom-call | tf_op jit(solution)/shard_map/triangular_solve | solution.py:125
  173.6 0.3 fusion.23
  173.9 0.3 convolution_subtract_fusion
  174.2 0.3 fusion.26
  174.5 0.4 fusion.13
  174.9 1.1 fusion.19
  176.1 5.9 %fusion.4 = bf16[255,2,48,128]{3,0,2,1:T(8,128)(2,1)S(1)} fusion(bf16[256,2,48,128]{3,2,1,0:T(8,128)(2,1)} %shard_map.31, bf16[255,255]{1,0:T(8,128)(2,1)S(1)} %fusion.20), kind=kOutput, calls=%fused_computation.5 | convolution fusion | flops 1607454720 | bytes 12688386 | tf_op jit(solution)/shard_map/dot_general | solution.py:172
  182.0 6.7 %copy.22 = bf16[255,2,48,128]{3,2,1,0:T(8,128)(2,1)} copy(bf16[255,2,48,128]{3,0,2,1:T(8,128)(2,1)S(1)} %fusion.4) | data formatting | bytes 12533760
  (36 shorter events, 0.7 us)
Async XLA Ops:
  8.6 12.7 %collective-permute-start.3 = (f32[8,48,128]{2,1,0:T(8,128)}, f32[8,48,128]{2,1,0:T(8,128)S(1)}, u32[]{:S(2)}, u32[]{:S(2)}) collective-permute-start(f32[8,48,128]{2,1,0:T(8,128)} %shard_map.30), channel_id=1, source_target_pairs={{1,0},{2,1},{3,2},{4,3},{5,4},{6,5},{7,6},{8,7},{9,8},{10,9},{11,1... | collective-permute-start | bytes 589832 | tf_op jit(solution)/shard_map/ppermute | solution.py:149
  11.2 10.0 %collective-permute-start.2 = (f32[8,48,128]{2,1,0:T(8,128)}, f32[8,48,128]{2,1,0:T(8,128)S(1)}, u32[]{:S(2)}, u32[]{:S(2)}) collective-permute-start(f32[8,48,128]{2,1,0:T(8,128)} %shard_map.30), channel_id=1, source_target_pairs={{0,1},{1,2},{2,3},{3,4},{4,5},{5,6},{6,7},{7,8},{8,9},{9,10},{10,1... | collective-permute-start | bytes 589832 | tf_op jit(solution)/shard_map/ppermute | solution.py:148
  18.6 3.4 %collective-permute-start = (f32[256,2,128]{2,1,0:T(2,128)S(1)}, f32[256,2,128]{2,1,0:T(2,128)S(1)}, u32[]{:S(2)}, u32[]{:S(2)}) collective-permute-start(f32[256,2,128]{2,1,0:T(2,128)S(1)} %get-tuple-element.26), channel_id=1, source_target_pairs={{0,16},{16,32},{32,48},{48,64},{64,80},{80,96},{96,112},{112,128},... | collective-permute-start | bytes 786440 | tf_op jit(solution)/shard_map/ppermute | solution.py:138
  19.9 5.6 %collective-permute-start.1 = (f32[256,2,128]{2,1,0:T(2,128)S(1)}, f32[256,2,128]{2,1,0:T(2,128)S(1)}, u32[]{:S(2)}, u32[]{:S(2)}) collective-permute-start(f32[256,2,128]{2,1,0:T(2,128)S(1)} %get-tuple-element.27), channel_id=1, source_target_pairs={{16,0},{32,16},{48,32},{64,48},{80,64},{96,80},{112,96},{128,112},... | collective-permute-start | bytes 786440 | tf_op jit(solution)/shard_map/ppermute | solution.py:139
  56.1 97.5 %copy-start = (f32[128,1]{1,0:T(8,128)S(1)}, f32[128,1]{1,0:T(8,128)}, u32[]{:S(2)}) copy-start(f32[128,1]{1,0:T(8,128)} %constant.117.clone.1) | copy-start | bytes 1540
  57.4 5.8 %collective-permute-start.4 = (f32[257,128]{1,0:T(8,128)S(1)}, f32[257,128]{1,0:T(8,128)S(1)}, u32[]{:S(2)}, u32[]{:S(2)}) collective-permute-start(f32[257,128]{1,0:T(8,128)S(1)} %pad_maximum_fusion.4), channel_id=1, source_target_pairs={{0,16},{16,0},{32,48},{48,32},{64,80},{80,64},{96,112},{112,96},{1... | collective-permute-start | bytes 394760 | tf_op jit(solution)/shard_map/ppermute | solution.py:119
  63.2 6.1 %collective-permute-start.5 = (f32[257,128]{1,0:T(8,128)S(1)}, f32[257,128]{1,0:T(8,128)S(1)}, u32[]{:S(2)}, u32[]{:S(2)}) collective-permute-start(f32[257,128]{1,0:T(8,128)S(1)} %fusion.35), channel_id=1, source_target_pairs={{0,32},{16,48},{32,0},{48,16},{64,96},{80,112},{96,64},{112,80},{1... | collective-permute-start | bytes 394760 | tf_op jit(solution)/shard_map/ppermute | solution.py:119
  69.4 12.2 %collective-permute-start.6 = (f32[257,128]{1,0:T(8,128)S(1)}, f32[257,128]{1,0:T(8,128)S(1)}, u32[]{:S(2)}, u32[]{:S(2)}) collective-permute-start(f32[257,128]{1,0:T(8,128)S(1)} %add.63), channel_id=1, source_target_pairs={{0,64},{16,80},{32,96},{48,112},{64,0},{80,16},{96,32},{112,48},{1... | collective-permute-start | bytes 394760 | tf_op jit(solution)/shard_map/ppermute | solution.py:119
  81.6 11.0 %collective-permute-start.7 = (f32[257,128]{1,0:T(8,128)S(1)}, f32[257,128]{1,0:T(8,128)S(1)}, u32[]{:S(2)}, u32[]{:S(2)}) collective-permute-start(f32[257,128]{1,0:T(8,128)S(1)} %add.64), channel_id=1, source_target_pairs={{0,128},{16,144},{32,160},{48,176},{64,192},{80,208},{96,224},{112... | collective-permute-start | bytes 394760 | tf_op jit(solution)/shard_map/ppermute | solution.py:119
  92.6 5.5 %collective-permute-start.8 = (f32[257,128]{1,0:T(8,128)S(1)}, f32[257,128]{1,0:T(8,128)S(1)}, u32[]{:S(2)}, u32[]{:S(2)}) collective-permute-start(f32[257,128]{1,0:T(8,128)S(1)} %add.65), channel_id=1, source_target_pairs={{0,1},{1,0},{2,3},{3,2},{4,5},{5,4},{6,7},{7,6},{8,9},{9,8},{10,11... | collective-permute-start | bytes 394760 | tf_op jit(solution)/shard_map/ppermute | solution.py:119
  98.1 6.6 %collective-permute-start.9 = (f32[257,128]{1,0:T(8,128)S(1)}, f32[257,128]{1,0:T(8,128)S(1)}, u32[]{:S(2)}, u32[]{:S(2)}) collective-permute-start(f32[257,128]{1,0:T(8,128)S(1)} %add.66), channel_id=1, source_target_pairs={{0,2},{1,3},{2,0},{3,1},{4,6},{5,7},{6,4},{7,5},{8,10},{9,11},{10,... | collective-permute-start | bytes 394760 | tf_op jit(solution)/shard_map/ppermute | solution.py:119
  104.8 5.1 %collective-permute-start.10 = (f32[257,128]{1,0:T(8,128)S(1)}, f32[257,128]{1,0:T(8,128)S(1)}, u32[]{:S(2)}, u32[]{:S(2)}) collective-permute-start(f32[257,128]{1,0:T(8,128)S(1)} %add.67), channel_id=1, source_target_pairs={{0,4},{1,5},{2,6},{3,7},{4,0},{5,1},{6,2},{7,3},{8,12},{9,13},{10,... | collective-permute-start | bytes 394760 | tf_op jit(solution)/shard_map/ppermute | solution.py:119
  109.9 6.8 %collective-permute-start.11 = (f32[257,128]{1,0:T(8,128)S(1)}, f32[257,128]{1,0:T(8,128)S(1)}, u32[]{:S(2)}, u32[]{:S(2)}) collective-permute-start(f32[257,128]{1,0:T(8,128)S(1)} %add.68), channel_id=1, source_target_pairs={{0,8},{1,9},{2,10},{3,11},{4,12},{5,13},{6,14},{7,15},{8,0},{9,1},... | collective-permute-start | bytes 394760 | tf_op jit(solution)/shard_map/ppermute | solution.py:119
where the time goes:
time: 189 us
  other arithmetic  58.7 us (31%)
  waiting for transfers between devices  41.9 us (22%)
  starting transfers between devices  31 us (16%)
  Pallas kernels  29.5 us (16%)
  matrix products  16.7 us (9%)
  local copies, waits for them, and re-layouts  8.6 us (5%)
  between operations  2.28 us (1%)
    ppermute x8, waiting for transfers between devices, doubling_sum(): lax.ppermute(value, axis, [(i, i ^ step) for i in range(count)])  38.4 us
    another operation x8, other arithmetic, shards(): lower = jnp.linalg.cholesky(gram[:snaps - 1, :snaps - 1])  34.5 us
    pallas_call x1, Pallas kernels, features_of(): pl.pallas_call(feature_kernel, grid=(snaps // block,), in_specs=[pl.Block...  21.6 us
    ppermute x8, starting transfers between devices, doubling_sum(): lax.ppermute(value, axis, [(i, i ^ step) for i in range(count)])  20.4 us
    another operation x4, other arithmetic, tri_solve(): return lax.linalg.triangular_solve(lower, right, left_side=True, lower=True)  20 us
    dot_general x1, matrix products, shards(): lax.dot_general(features, features, (((1, 2, 3), (1, 2, 3)), ((), ())), p...  7.98 us
    pallas_call x1, Pallas kernels, edges_of(): pl.pallas_call(edge_kernel, grid=(snaps // block,), in_specs=[pl.BlockSpe...  7.92 us
    unnamed x3, local copies, waits for them, and re-layouts  6.75 us
  transfers between devices with their start and end apart: 12, of which 9 were waited for; matrix products, arithmetic and copies ran while one was open for 2% of the time, Pallas kernels for 0%

commit v1 on v0

--- a/solution.py
+++ b/solution.py
@@ -1,3 +1,4 @@
+import numpy as np
 import jax
 import jax.numpy as jnp
 from jax import lax
@@ -112,6 +113,27 @@
     )
 
 
+def lower_slots(rows, cols, width):
+    taken = [(i, j) for i in range(rows) for j in range(cols) if j <= i]
+    flat = np.array([i * cols + j for i, j in taken], np.int32)
+    length = -(-len(flat) // width) * width
+    picks = np.zeros(length, np.int32)
+    picks[: len(flat)] = flat
+    spot = {pair: n for n, pair in enumerate(taken)}
+    back = np.array([[spot[max(i, j), min(i, j)] for j in range(cols)] for i in range(rows)], np.int32)
+    return picks, back
+
+
+def pack_lower(block, width):
+    picks, _ = lower_slots(block.shape[0], block.shape[1], width)
+    return block.reshape(-1)[picks].reshape(-1, width)
+
+
+def unpack_lower(packed, size):
+    _, back = lower_slots(size, size, packed.shape[1])
+    return packed.reshape(-1)[back]
+
+
 def doubling_sum(value, axis):
     count = lax.axis_size(axis)
     step = 1
@@ -159,12 +181,41 @@
         )
         / total_rows
     )
-    packed = doubling_sum(doubling_sum(pack_symmetric(local_gram), "gx"), "gy")
-    gram = unpack_symmetric(packed)
-    lower = jnp.linalg.cholesky(gram[: snaps - 1, : snaps - 1])
-    cross = gram[: snaps - 1, 1:]
-    inverse = tri_solve(lower, jnp.eye(snaps - 1, dtype=jnp.float32))
+    half = snaps // 2
+    lead = unpack_lower(
+        doubling_sum(doubling_sum(pack_lower(local_gram[:half, :half], half), "gx"), "gy"), half
+    )
+    rest = doubling_sum(
+        doubling_sum(
+            jnp.concatenate(
+                [local_gram[half:, :half], pack_lower(local_gram[half:, half:], half)], axis=0
+            ),
+            "gx",
+        ),
+        "gy",
+    )
+    side = rest[:half]
+    corner = unpack_lower(rest[half:], half)
+    gram = jnp.concatenate(
+        [jnp.concatenate([lead, side.T], axis=1), jnp.concatenate([side, corner], axis=1)], axis=0
+    )
     highest = lax.Precision.HIGHEST
+    size = snaps - 1
+    low11 = jnp.linalg.cholesky(lead)
+    inv11 = tri_solve(low11, jnp.eye(half, dtype=jnp.float32))
+    low21 = jnp.dot(side[: size - half], inv11.T, precision=highest)
+    schur = corner[: size - half, : size - half] - jnp.dot(low21, low21.T, precision=highest)
+    low22 = jnp.linalg.cholesky(schur)
+    inv22 = tri_solve(low22, jnp.eye(size - half, dtype=jnp.float32))
+    inv21 = -jnp.dot(inv22, jnp.dot(low21, inv11, precision=highest), precision=highest)
+    inverse = jnp.concatenate(
+        [
+            jnp.concatenate([inv11, jnp.zeros((half, size - half), jnp.float32)], axis=1),
+            jnp.concatenate([inv21, inv22], axis=1),
+        ],
+        axis=0,
+    )
+    cross = gram[:size, 1:]
     reduced = jnp.dot(jnp.dot(inverse, cross, precision=highest), inverse.T, precision=highest)
     shifted = jnp.concatenate(
         [jnp.zeros((snaps - 1, 1), jnp.bfloat16), inverse.astype(jnp.bfloat16)], axis=1

time: 189 us -> 458 us (2.42); the launches traced: 189 us -> 449 us
  local copies, waits for them, and re-layouts: 8.6 us -> 275 us
  other arithmetic: 58.7 us -> 49.6 us
  starting transfers between devices: 31 us -> 38.1 us
    gather x1 -> x5, local copies, waits for them, and re-layouts: 1.25 us -> 268 us  [the longest x3 181 us: unpack_lower(): return packed.reshape(-1)[back]]
    another operation x8 -> x6, other arithmetic: 34.5 us -> 24.7 us  [the longest x3 12.4 us: shards(): low11 = jnp.linalg.cholesky(lead)]
    ppermute x8 -> x16, starting transfers between devices: 20.4 us -> 27.6 us  [doubling_sum(): lax.ppermute(value, axis, [(i, i ^ step) for i in range(count)])]
    ppermute x8 -> x16, waiting for transfers between devices: 38.4 us -> 34.8 us  [doubling_sum(): lax.ppermute(value, axis, [(i, i ^ step) for i in range(count)])]
  transfers between devices with their start and end apart: 12 -> 20, of which waited for: 9 -> 11; matrix products, arithmetic and copies ran while one was open for 2% -> 36% of each run, Pallas kernels for 0% -> 0%
where the time goes in v1:
time: 458 us; the launch traced here: 449 us
  local copies, waits for them, and re-layouts  275 us (60%)
  other arithmetic  49.6 us (11%)
  waiting for transfers between devices  38.3 us (8%)
  starting transfers between devices  38.1 us (8%)
  Pallas kernels  29.5 us (6%)
  matrix products  17.1 us (4%)
    gather x3, local copies, waits for them, and re-layouts, unpack_lower(): return packed.reshape(-1)[back]  181 us
    gather x2, local copies, waits for them, and re-layouts, pack_lower(): return block.reshape(-1)[picks].reshape(-1, width)  86.2 us
    ppermute x16, waiting for transfers between devices, doubling_sum(): lax.ppermute(value, axis, [(i, i ^ step) for i in range(count)])  34.8 us
    ppermute x16, starting transfers between devices, doubling_sum(): lax.ppermute(value, axis, [(i, i ^ step) for i in range(count)])  27.6 us
    pallas_call x1, Pallas kernels, features_of(): pl.pallas_call(feature_kernel, grid=(snaps // block,), in_specs=[pl.Block...  21.6 us
    another operation x4, other arithmetic, tri_solve(): return lax.linalg.triangular_solve(lower, right, left_side=True, lower=True)  20.9 us
    another operation x3, other arithmetic, shards(): low11 = jnp.linalg.cholesky(lead)  12.4 us
    another operation x3, other arithmetic, shards(): low22 = jnp.linalg.cholesky(schur)  12.3 us
  transfers between devices with their start and end apart: 20, of which 11 were waited for; matrix products, arithmetic and copies ran while one was open for 36% of the time, Pallas kernels for 0%

profile of v1, /device:TPU:24, one launch (start us, length us, event | category | flops | bytes accessed | tf_op | source)
XLA Modules:
  0.0 449.0 jit_solution(12600615278309633164)
XLA Ops:
  0.6 7.9 %shard_map.104 = f32[8,48,128]{2,1,0:T(8,128)} custom-call(bf16[2,256,48,128]{3,2,1,0:T(8,128)(2,1)} %ener_ref.3, bf16[2,256,48,128]{3,2,1,0:T(8,128)(2,1)} %ener_ref.3), custom_call_target="tpu_custom_call" | custom-call | tf_op jit(solution)/shard_map/pallas_call | solution.py:73
  8.6 2.6 collective-permute-start.3
  11.2 5.3 %collective-permute-start.2 = (f32[8,48,128]{2,1,0:T(8,128)}, f32[8,48,128]{2,1,0:T(8,128)S(1)}, u32[]{:S(2)}, u32[]{:S(2)}) collective-permute-start(f32[8,48,128]{2,1,0:T(8,128)} %shard_map.104), channel_id=1, source_target_pairs={{0,1},{1,2},{2,3},{3,4},{4,5},{5,6},{6,7},{7,8},{8,9},{9,10},{10,1... | collective-permute-start | bytes 589832 | tf_op jit(solution)/shard_map/ppermute | solution.py:170
  16.5 2.0 fusion.19
  18.6 1.3 collective-permute-start
  19.9 1.3 collective-permute-start.1
  21.3 0.7 fusion.20.yh_ref
  22.0 3.5 collective-permute-done.1
  25.5 1.0 pad_maximum_fusion.xh_ref
  26.5 21.6 %shard_map.105 = bf16[256,2,48,128]{3,2,1,0:T(8,128)(2,1)} custom-call(bf16[2,256,48,128]{3,2,1,0:T(8,128)(2,1)} %ener_ref.3, bf16[2,256,48,128]{3,2,1,0:T(8,128)(2,1)} %ener_ref.3, f32[256,4,128]{2,1,0:T(4,128)} %pad_maximum_fusion.xh_ref, f32[8,48,128]{2,1,0:T(8,128)} %fusion.20.yh_ref), custom_call_target="tpu_custom_call" | custom-call | tf_op jit(solution)/shard_map/pallas_call | solution.py:44
  48.1 8.0 %fusion.10 = f32[256,256]{1,0:T(8,128)S(1)} fusion(bf16[256,2,48,128]{3,2,1,0:T(8,128)(2,1)} %shard_map.105), kind=kOutput, calls=%fused_computation.10 | convolution fusion | flops 1610678272 | bytes 6553600 | tf_op jit(solution)/shard_map/dot_general | solution.py:179
  56.1 43.1 %gather_fusion = f32[8320]{0:T(1024)S(1)} fusion(f32[16384]{0:T(1024)S(1)} %get-tuple-element.8, s32[9216]{0:T(1024)S(1)} %pad_clamp_fusion), kind=kCustom, calls=%fused_computation | custom fusion | bytes 99840 | tf_op jit(solution)/shard_map/gather | solution.py:129
  99.2 4.8 %collective-permute-start.4 = (f32[65,128]{1,0:T(8,128)S(1)}, f32[65,128]{1,0:T(8,128)S(1)}, u32[]{:S(2)}, u32[]{:S(2)}) collective-permute-start(f32[65,128]{1,0:T(8,128)S(1)} %bitcast.63), channel_id=1, source_target_pairs={{0,16},{16,0},{32,48},{48,32},{64,80},{80,64},{96,112},{112,96},{1... | collective-permute-start | bytes 99848 | tf_op jit(solution)/shard_map/ppermute | solution.py:141
  104.1 0.9 collective-permute-done.4
  104.9 1.9 collective-permute-start.5
  106.8 2.0 collective-permute-done.5
  108.9 5.7 %collective-permute-start.6 = (f32[65,128]{1,0:T(8,128)S(1)}, f32[65,128]{1,0:T(8,128)S(1)}, u32[]{:S(2)}, u32[]{:S(2)}) collective-permute-start(f32[65,128]{1,0:T(8,128)S(1)} %fusion.52), channel_id=1, source_target_pairs={{0,64},{16,80},{32,96},{48,112},{64,0},{80,16},{96,32},{112,48},{1... | collective-permute-start | bytes 99848 | tf_op jit(solution)/shard_map/ppermute | solution.py:141
  114.6 43.1 %gather_fusion.2 = f32[8320]{0:T(1024)S(1)} fusion(f32[16384]{0:T(1024)S(1)} %get-tuple-element.9, s32[9216]{0:T(1024)S(1)} %pad_clamp_fusion), kind=kCustom, calls=%fused_computation.2 | custom fusion | bytes 99840 | tf_op jit(solution)/shard_map/gather | solution.py:129
  157.8 2.2 collective-permute-start.7
  160.1 5.6 %collective-permute-done.7 = f32[65,128]{1,0:T(8,128)S(1)} collective-permute-done((f32[65,128]{1,0:T(8,128)S(1)}, f32[65,128]{1,0:T(8,128)S(1)}, u32[]{:S(2)}, u32[]{:S(2)}) %collective-permute-start.7) | collective-permute-done | bytes 33312 | tf_op jit(solution)/shard_map/ppermute | solution.py:141
  165.7 3.9 collective-permute-done.8
  169.7 5.5 %collective-permute-done.9 = f32[65,128]{1,0:T(8,128)S(1)} collective-permute-done((f32[65,128]{1,0:T(8,128)S(1)}, f32[65,128]{1,0:T(8,128)S(1)}, u32[]{:S(2)}, u32[]{:S(2)}) %collective-permute-start.9) | collective-permute-done | bytes 33312 | tf_op jit(solution)/shard_map/ppermute | solution.py:141
  175.1 1.5 collective-permute-start.10
  176.7 2.1 collective-permute-start.13
  178.7 0.4 collective-permute-done.10
  179.1 3.0 collective-permute-start.11
  182.5 2.1 collective-permute-done.11
  184.6 90.5 %gather_fusion.1 = f32[16384]{0:T(1024)S(1)} fusion(f32[8320]{0:T(1024)S(1)} %add_bitcast_fusion, s32[16384]{0:T(1024)S(1)} %broadcast_clamp_fusion), kind=kCustom, calls=%fused_computation.1 | custom fusion | bytes 196608 | tf_op jit(solution)/shard_map/gather | solution.py:134
  275.2 2.3 collective-permute-start.15
  277.6 11.7 %cholesky.31 = f32[128,128]{1,0:T(8,128)S(1)} custom-call(f32[128,128]{1,0:T(8,128)S(1)} %fusion.34), custom_call_target="Cholesky" | custom-call | tf_op jit(solution)/shard_map/jit(cholesky)/cholesky | solution.py:204
  289.6 4.4 collective-permute-done.16
  294.2 0.6 compare_reduce_fusion.1
  294.8 5.5 %collective-permute-done.17 = f32[193,128]{1,0:T(8,128)S(1)} collective-permute-done((f32[193,128]{1,0:T(8,128)S(1)}, f32[193,128]{1,0:T(8,128)S(1)}, u32[]{:S(2)}, u32[]{:S(2)}) %collective-permute-start.17) | collective-permute-done | bytes 98848 | tf_op jit(solution)/shard_map/ppermute | solution.py:141
  300.4 1.6 collective-permute-start.18
  301.9 0.7 fusion.25
  302.6 9.8 %custom-call.12 = f32[1,128,128]{1,2,0:T(8,128)S(1)} custom-call(f32[1,128,128]{2,1,0:T(8,128)S(1)} %fusion.25), custom_call_target="InvertDiagBlocksLowerTriangular" | custom-call | tf_op jit(solution)/shard_map/triangular_solve | solution.py:147
  312.4 1.6 collective-permute-start.19
  314.3 4.4 collective-permute-done.19
  318.7 90.7 %gather_fusion.3 = f32[16384]{0:T(1024)S(1)} fusion(f32[8320]{0:T(1024)S(1)} %slice_bitcast_fusion.2, s32[16384]{0:T(1024)S(1)} %broadcast_clamp_fusion), kind=kCustom, calls=%fused_computation.3 | custom fusion | bytes 196608 | tf_op jit(solution)/shard_map/gather | solution.py:134
  410.6 11.6 %cholesky.65 = f32[127,127]{1,0:T(8,128)S(1)} custom-call(f32[127,127]{1,0:T(8,128)S(1)} %fusion.31), custom_call_target="Cholesky" | custom-call | tf_op jit(solution)/shard_map/jit(cholesky)/cholesky | solution.py:208
  422.3 0.6 compare_reduce_fusion
  422.9 0.7 fusion.26
  423.6 9.7 %custom-call.13 = f32[1,127,127]{1,2,0:T(8,128)S(1)} custom-call(f32[1,127,127]{2,1,0:T(8,128)S(1)} %fusion.26), custom_call_target="InvertDiagBlocksLowerTriangular" | custom-call | tf_op jit(solution)/shard_map/triangular_solve | solution.py:147
  433.7 0.3 convolution_negate_fusion
  434.0 0.5 fusion.14
  434.5 1.1 fusion.23
  435.6 5.9 %fusion.4 = bf16[255,2,48,128]{3,0,2,1:T(8,128)(2,1)S(1)} fusion(bf16[256,2,48,128]{3,2,1,0:T(8,128)(2,1)} %shard_map.105, bf16[255,255]{1,0:T(8,128)(2,1)S(1)} %fusion.24), kind=kOutput, calls=%fused_computation.8 | convolution fusion | flops 1607454720 | bytes 12688386 | tf_op jit(solution)/shard_map/dot_general | solution.py:223
  441.6 7.0 %copy.30 = bf16[255,2,48,128]{3,2,1,0:T(8,128)(2,1)} copy(bf16[255,2,48,128]{3,0,2,1:T(8,128)(2,1)S(1)} %fusion.4) | data formatting | bytes 12533760
  (58 shorter events, 2.9 us)
Async XLA Ops:
  0.6 20.6 %copy-start.1 = (s32[8320]{0:T(1024)S(1)}, s32[8320]{0:T(1024)}, u32[]{:S(2)}) copy-start(s32[8320]{0:T(1024)} %constant.124) | copy-start | bytes 99844
  8.6 12.7 %collective-permute-start.3 = (f32[8,48,128]{2,1,0:T(8,128)}, f32[8,48,128]{2,1,0:T(8,128)S(1)}, u32[]{:S(2)}, u32[]{:S(2)}) collective-permute-start(f32[8,48,128]{2,1,0:T(8,128)} %shard_map.104), channel_id=1, source_target_pairs={{1,0},{2,1},{3,2},{4,3},{5,4},{6,5},{7,6},{8,7},{9,8},{10,9},{11,1... | collective-permute-start | bytes 589832 | tf_op jit(solution)/shard_map/ppermute | solution.py:171
  11.2 10.0 %collective-permute-start.2 = (f32[8,48,128]{2,1,0:T(8,128)}, f32[8,48,128]{2,1,0:T(8,128)S(1)}, u32[]{:S(2)}, u32[]{:S(2)}) collective-permute-start(f32[8,48,128]{2,1,0:T(8,128)} %shard_map.104), channel_id=1, source_target_pairs={{0,1},{1,2},{2,3},{3,4},{4,5},{5,6},{6,7},{7,8},{8,9},{9,10},{10,1... | collective-permute-start | bytes 589832 | tf_op jit(solution)/shard_map/ppermute | solution.py:170
  18.6 3.4 collective-permute-start
  19.9 5.6 %collective-permute-start.1 = (f32[256,2,128]{2,1,0:T(2,128)S(1)}, f32[256,2,128]{2,1,0:T(2,128)S(1)}, u32[]{:S(2)}, u32[]{:S(2)}) collective-permute-start(f32[256,2,128]{2,1,0:T(2,128)S(1)} %get-tuple-element.7), channel_id=1, source_target_pairs={{16,0},{32,16},{48,32},{64,48},{80,64},{96,80},{112,96},{128,112},... | collective-permute-start | bytes 786440 | tf_op jit(solution)/shard_map/ppermute | solution.py:161
  99.2 5.7 %collective-permute-start.4 = (f32[65,128]{1,0:T(8,128)S(1)}, f32[65,128]{1,0:T(8,128)S(1)}, u32[]{:S(2)}, u32[]{:S(2)}) collective-permute-start(f32[65,128]{1,0:T(8,128)S(1)} %bitcast.63), channel_id=1, source_target_pairs={{0,16},{16,0},{32,48},{48,32},{64,80},{80,64},{96,112},{112,96},{1... | collective-permute-start | bytes 99848 | tf_op jit(solution)/shard_map/ppermute | solution.py:141
  104.9 4.0 collective-permute-start.5
  108.9 48.8 %collective-permute-start.6 = (f32[65,128]{1,0:T(8,128)S(1)}, f32[65,128]{1,0:T(8,128)S(1)}, u32[]{:S(2)}, u32[]{:S(2)}) collective-permute-start(f32[65,128]{1,0:T(8,128)S(1)} %fusion.52), channel_id=1, source_target_pairs={{0,64},{16,80},{32,96},{48,112},{64,0},{80,16},{96,32},{112,48},{1... | collective-permute-start | bytes 99848 | tf_op jit(solution)/shard_map/ppermute | solution.py:141
  114.6 67.5 %copy-start = (s32[16384]{0:T(1024)S(1)}, s32[16384]{0:T(1024)}, u32[]{:S(2)}) copy-start(s32[16384]{0:T(1024)} %constant.125) | copy-start | bytes 196612
  157.8 8.0 %collective-permute-start.7 = (f32[65,128]{1,0:T(8,128)S(1)}, f32[65,128]{1,0:T(8,128)S(1)}, u32[]{:S(2)}, u32[]{:S(2)}) collective-permute-start(f32[65,128]{1,0:T(8,128)S(1)} %add.97), channel_id=1, source_target_pairs={{0,128},{16,144},{32,160},{48,176},{64,192},{80,208},{96,224},{112... | collective-permute-start | bytes 99848 | tf_op jit(solution)/shard_map/ppermute | solution.py:141
  160.0 16.7 %collective-permute-start.12 = (f32[193,128]{1,0:T(8,128)S(1)}, f32[193,128]{1,0:T(8,128)S(1)}, u32[]{:S(2)}, u32[]{:S(2)}) collective-permute-start(f32[193,128]{1,0:T(8,128)S(1)} %pad_maximum_fusion.4), channel_id=1, source_target_pairs={{0,16},{16,0},{32,48},{48,32},{64,80},{80,64},{96,112},{112,96},{1... | collective-permute-start | bytes 296456 | tf_op jit(solution)/shard_map/ppermute | solution.py:141
  165.7 4.0 collective-permute-start.8
  169.7 5.5 %collective-permute-start.9 = (f32[65,128]{1,0:T(8,128)S(1)}, f32[65,128]{1,0:T(8,128)S(1)}, u32[]{:S(2)}, u32[]{:S(2)}) collective-permute-start(f32[65,128]{1,0:T(8,128)S(1)} %add.99), channel_id=1, source_target_pairs={{0,2},{1,3},{2,0},{3,1},{4,6},{5,7},{6,4},{7,5},{8,10},{9,11},{10,... | collective-permute-start | bytes 99848 | tf_op jit(solution)/shard_map/ppermute | solution.py:141
  175.1 4.0 collective-permute-start.10
  176.7 5.5 %collective-permute-start.13 = (f32[193,128]{1,0:T(8,128)S(1)}, f32[193,128]{1,0:T(8,128)S(1)}, u32[]{:S(2)}, u32[]{:S(2)}) collective-permute-start(f32[193,128]{1,0:T(8,128)S(1)} %fusion.42), channel_id=1, source_target_pairs={{0,32},{16,48},{32,0},{48,16},{64,96},{80,112},{96,64},{112,80},{1... | collective-permute-start | bytes 296456 | tf_op jit(solution)/shard_map/ppermute | solution.py:141
  179.1 5.5 %collective-permute-start.11 = (f32[65,128]{1,0:T(8,128)S(1)}, f32[65,128]{1,0:T(8,128)S(1)}, u32[]{:S(2)}, u32[]{:S(2)}) collective-permute-start(f32[65,128]{1,0:T(8,128)S(1)} %add.101), channel_id=1, source_target_pairs={{0,8},{1,9},{2,10},{3,11},{4,12},{5,13},{6,14},{7,15},{8,0},{9,1},... | collective-permute-start | bytes 99848 | tf_op jit(solution)/shard_map/ppermute | solution.py:141
  182.2 93.0 %collective-permute-start.14 = (f32[193,128]{1,0:T(8,128)S(1)}, f32[193,128]{1,0:T(8,128)S(1)}, u32[]{:S(2)}, u32[]{:S(2)}) collective-permute-start(f32[193,128]{1,0:T(8,128)S(1)} %add.107), channel_id=1, source_target_pairs={{0,64},{16,80},{32,96},{48,112},{64,0},{80,16},{96,32},{112,48},{1... | collective-permute-start | bytes 296456 | tf_op jit(solution)/shard_map/ppermute | solution.py:141
  275.2 14.0 %collective-permute-start.15 = (f32[193,128]{1,0:T(8,128)S(1)}, f32[193,128]{1,0:T(8,128)S(1)}, u32[]{:S(2)}, u32[]{:S(2)}) collective-permute-start(f32[193,128]{1,0:T(8,128)S(1)} %add.108), channel_id=1, source_target_pairs={{0,128},{16,144},{32,160},{48,176},{64,192},{80,208},{96,224},{112... | collective-permute-start | bytes 296456 | tf_op jit(solution)/shard_map/ppermute | solution.py:141
  289.3 4.7 %collective-permute-start.16 = (f32[193,128]{1,0:T(8,128)S(1)}, f32[193,128]{1,0:T(8,128)S(1)}, u32[]{:S(2)}, u32[]{:S(2)}) collective-permute-start(f32[193,128]{1,0:T(8,128)S(1)} %add.109), channel_id=1, source_target_pairs={{0,1},{1,0},{2,3},{3,2},{4,5},{5,4},{6,7},{7,6},{8,9},{9,8},{10,11... | collective-permute-start | bytes 296456 | tf_op jit(solution)/shard_map/ppermute | solution.py:141
  294.1 6.3 %collective-permute-start.17 = (f32[193,128]{1,0:T(8,128)S(1)}, f32[193,128]{1,0:T(8,128)S(1)}, u32[]{:S(2)}, u32[]{:S(2)}) collective-permute-start(f32[193,128]{1,0:T(8,128)S(1)} %add.110), channel_id=1, source_target_pairs={{0,2},{1,3},{2,0},{3,1},{4,6},{5,7},{6,4},{7,5},{8,10},{9,11},{10,... | collective-permute-start | bytes 296456 | tf_op jit(solution)/shard_map/ppermute | solution.py:141
  300.4 12.1 %collective-permute-start.18 = (f32[193,128]{1,0:T(8,128)S(1)}, f32[193,128]{1,0:T(8,128)S(1)}, u32[]{:S(2)}, u32[]{:S(2)}) collective-permute-start(f32[193,128]{1,0:T(8,128)S(1)} %add.111), channel_id=1, source_target_pairs={{0,4},{1,5},{2,6},{3,7},{4,0},{5,1},{6,2},{7,3},{8,12},{9,13},{10,... | collective-permute-start | bytes 296456 | tf_op jit(solution)/shard_map/ppermute | solution.py:141
  312.4 6.3 %collective-permute-start.19 = (f32[193,128]{1,0:T(8,128)S(1)}, f32[193,128]{1,0:T(8,128)S(1)}, u32[]{:S(2)}, u32[]{:S(2)}) collective-permute-start(f32[193,128]{1,0:T(8,128)S(1)} %add.112), channel_id=1, source_target_pairs={{0,8},{1,9},{2,10},{3,11},{4,12},{5,13},{6,14},{7,15},{8,0},{9,1},... | collective-permute-start | bytes 296456 | tf_op jit(solution)/shard_map/ppermute | solution.py:141

commit v2 on v0

--- a/solution.py
+++ b/solution.py
@@ -159,12 +159,32 @@
         )
         / total_rows
     )
-    packed = doubling_sum(doubling_sum(pack_symmetric(local_gram), "gx"), "gy")
-    gram = unpack_symmetric(packed)
-    lower = jnp.linalg.cholesky(gram[: snaps - 1, : snaps - 1])
-    cross = gram[: snaps - 1, 1:]
-    inverse = tri_solve(lower, jnp.eye(snaps - 1, dtype=jnp.float32))
+    half = snaps // 2
+    packed = pack_symmetric(local_gram)
+    folded = doubling_sum(doubling_sum(packed[half : 2 * half], "gx"), "gy")
+    edge = jnp.concatenate([packed[:half], packed[2 * half :]], axis=0)
+    edge = doubling_sum(doubling_sum(edge, "gx"), "gy")
+    side = edge[:half]
+    gram = unpack_symmetric(jnp.concatenate([side, folded, edge[half:]], axis=0))
+    lead = gram[:half, :half]
+    corner = gram[half:, half:]
     highest = lax.Precision.HIGHEST
+    size = snaps - 1
+    low11 = jnp.linalg.cholesky(lead)
+    inv11 = tri_solve(low11, jnp.eye(half, dtype=jnp.float32))
+    low21 = jnp.dot(side[: size - half], inv11.T, precision=highest)
+    schur = corner[: size - half, : size - half] - jnp.dot(low21, low21.T, precision=highest)
+    low22 = jnp.linalg.cholesky(schur)
+    inv22 = tri_solve(low22, jnp.eye(size - half, dtype=jnp.float32))
+    inv21 = -jnp.dot(inv22, jnp.dot(low21, inv11, precision=highest), precision=highest)
+    inverse = jnp.concatenate(
+        [
+            jnp.concatenate([inv11, jnp.zeros((half, size - half), jnp.float32)], axis=1),
+            jnp.concatenate([inv21, inv22], axis=1),
+        ],
+        axis=0,
+    )
+    cross = gram[:size, 1:]
     reduced = jnp.dot(jnp.dot(inverse, cross, precision=highest), inverse.T, precision=highest)
     shifted = jnp.concatenate(
         [jnp.zeros((snaps - 1, 1), jnp.bfloat16), inverse.astype(jnp.bfloat16)], axis=1

time: 189 us -> 172 us (0.910)
  waiting for transfers between devices: 41.9 us -> 24.5 us
  starting transfers between devices: 31 us -> 41.4 us
  other arithmetic: 58.7 us -> 49.9 us
    ppermute x8 -> x16, waiting for transfers between devices: 38.4 us -> 21 us  [doubling_sum(): lax.ppermute(value, axis, [(i, i ^ step) for i in range(count)])]
    ppermute x8 -> x16, starting transfers between devices: 20.4 us -> 30.8 us  [doubling_sum(): lax.ppermute(value, axis, [(i, i ^ step) for i in range(count)])]
    another operation x8 -> x7, other arithmetic: 34.5 us -> 24.7 us  [the longest x4 12.4 us: shards(): low11 = jnp.linalg.cholesky(lead)]
    unnamed x3 -> x1, local copies, waits for them, and re-layouts: 6.75 us -> 6.74 us
  transfers between devices with their start and end apart: 12 -> 20, of which waited for: 9 -> 10; matrix products, arithmetic and copies ran while one was open for 2% -> 15% of each run, Pallas kernels for 0% -> 0%
where the time goes in v2:
time: 172 us
  other arithmetic  49.9 us (29%)
  starting transfers between devices  41.4 us (24%)
  Pallas kernels  29.5 us (17%)
  waiting for transfers between devices  24.5 us (14%)
  matrix products  17 us (10%)
  local copies, waits for them, and re-layouts  8.68 us (5%)
    ppermute x16, starting transfers between devices, doubling_sum(): lax.ppermute(value, axis, [(i, i ^ step) for i in range(count)])  30.8 us
    pallas_call x1, Pallas kernels, features_of(): pl.pallas_call(feature_kernel, grid=(snaps // block,), in_specs=[pl.Block...  21.6 us
    another operation x4, other arithmetic, tri_solve(): return lax.linalg.triangular_solve(lower, right, left_side=True, lower=True)  21.1 us
    ppermute x16, waiting for transfers between devices, doubling_sum(): lax.ppermute(value, axis, [(i, i ^ step) for i in range(count)])  21 us
    another operation x4, other arithmetic, shards(): low11 = jnp.linalg.cholesky(lead)  12.4 us
    another operation x3, other arithmetic, shards(): low22 = jnp.linalg.cholesky(schur)  12.3 us
    dot_general x1, matrix products, shards(): lax.dot_general(features, features, (((1, 2, 3), (1, 2, 3)), ((), ())), p...  7.98 us
    pallas_call x1, Pallas kernels, edges_of(): pl.pallas_call(edge_kernel, grid=(snaps // block,), in_specs=[pl.BlockSpe...  7.92 us
  transfers between devices with their start and end apart: 20, of which 10 were waited for; matrix products, arithmetic and copies ran while one was open for 15% of the time, Pallas kernels for 0%

profile of v2, /device:TPU:24, one launch (start us, length us, event | category | flops | bytes accessed | tf_op | source)
XLA Modules:
  0.0 172.0 jit_solution(2575596590895739369)
XLA Ops:
  0.6 7.9 %shard_map.30 = f32[8,48,128]{2,1,0:T(8,128)} custom-call(bf16[2,256,48,128]{3,2,1,0:T(8,128)(2,1)} %ener_ref.3, bf16[2,256,48,128]{3,2,1,0:T(8,128)(2,1)} %ener_ref.3), custom_call_target="tpu_custom_call" | custom-call | tf_op jit(solution)/shard_map/pallas_call | solution.py:72
  8.6 2.6 %collective-permute-start.3 = (f32[8,48,128]{2,1,0:T(8,128)}, f32[8,48,128]{2,1,0:T(8,128)S(1)}, u32[]{:S(2)}, u32[]{:S(2)}) collective-permute-start(f32[8,48,128]{2,1,0:T(8,128)} %shard_map.30), channel_id=1, source_target_pairs={{1,0},{2,1},{3,2},{4,3},{5,4},{6,5},{7,6},{8,7},{9,8},{10,9},{11,1... | collective-permute-start | bytes 589832 | tf_op jit(solution)/shard_map/ppermute | solution.py:149
  11.2 5.3 %collective-permute-start.2 = (f32[8,48,128]{2,1,0:T(8,128)}, f32[8,48,128]{2,1,0:T(8,128)S(1)}, u32[]{:S(2)}, u32[]{:S(2)}) collective-permute-start(f32[8,48,128]{2,1,0:T(8,128)} %shard_map.30), channel_id=1, source_target_pairs={{0,1},{1,2},{2,3},{3,4},{4,5},{5,6},{6,7},{7,8},{8,9},{9,10},{10,1... | collective-permute-start | bytes 589832 | tf_op jit(solution)/shard_map/ppermute | solution.py:148
  16.5 2.0 %fusion.19 = (f32[256,2,128]{2,1,0:T(2,128)S(1)}, f32[256,2,128]{2,1,0:T(2,128)S(1)}) fusion(bf16[2,256,48,128]{3,2,1,0:T(8,128)(2,1)} %ener_ref.3), kind=kLoop, calls=%fused_computation.21 | loop fusion | flops 524288 | bytes 1048576 | tf_op jit(solution)/shard_map/div | solution.py:134
  18.6 1.3 collective-permute-start
  19.9 1.3 collective-permute-start.1
  21.2 0.7 fusion.20.yh_ref
  21.9 3.5 %collective-permute-done.1 = f32[256,2,128]{2,1,0:T(2,128)S(1)} collective-permute-done((f32[256,2,128]{2,1,0:T(2,128)S(1)}, f32[256,2,128]{2,1,0:T(2,128)S(1)}, u32[]{:S(2)}, u32[]{:S(2)}) %collective-permute-start.1) | collective-permute-done | bytes 262176 | tf_op jit(solution)/shard_map/ppermute | solution.py:139
  25.4 1.0 pad_maximum_fusion.xh_ref
  26.5 21.6 %shard_map.31 = bf16[256,2,48,128]{3,2,1,0:T(8,128)(2,1)} custom-call(bf16[2,256,48,128]{3,2,1,0:T(8,128)(2,1)} %ener_ref.3, bf16[2,256,48,128]{3,2,1,0:T(8,128)(2,1)} %ener_ref.3, f32[256,4,128]{2,1,0:T(4,128)} %pad_maximum_fusion.xh_ref, f32[8,48,128]{2,1,0:T(8,128)} %fusion.20.yh_ref), custom_call_target="tpu_custom_call" | custom-call | tf_op jit(solution)/shard_map/pallas_call | solution.py:43
  48.1 8.0 %fusion.10 = f32[256,256]{1,0:T(8,128)S(1)} fusion(bf16[256,2,48,128]{3,2,1,0:T(8,128)(2,1)} %shard_map.31), kind=kOutput, calls=%fused_computation.7 | convolution fusion | flops 1610678272 | bytes 6553600 | tf_op jit(solution)/shard_map/dot_general | solution.py:157
  56.1 1.2 gather_fusion
  57.4 4.8 %collective-permute-start.12 = (f32[129,128]{1,0:T(8,128)S(1)}, f32[129,128]{1,0:T(8,128)S(1)}, u32[]{:S(2)}, u32[]{:S(2)}) collective-permute-start(f32[129,128]{1,0:T(8,128)S(1)} %pad_maximum_fusion.4), channel_id=1, source_target_pairs={{0,16},{16,0},{32,48},{48,32},{64,80},{80,64},{96,112},{112,96},{1... | collective-permute-start | bytes 198152 | tf_op jit(solution)/shard_map/ppermute | solution.py:119
  62.3 1.2 collective-permute-done.4
  63.5 2.0 %collective-permute-start.5 = (f32[128,128]{1,0:T(8,128)S(1)}, f32[128,128]{1,0:T(8,128)S(1)}, u32[]{:S(2)}, u32[]{:S(2)}) collective-permute-start(f32[128,128]{1,0:T(8,128)S(1)} %add.86), channel_id=1, source_target_pairs={{0,32},{16,48},{32,0},{48,16},{64,96},{80,112},{96,64},{112,80},{1... | collective-permute-start | bytes 196616 | tf_op jit(solution)/shard_map/ppermute | solution.py:119
  65.7 2.2 %collective-permute-done.5 = f32[128,128]{1,0:T(8,128)S(1)} collective-permute-done((f32[128,128]{1,0:T(8,128)S(1)}, f32[128,128]{1,0:T(8,128)S(1)}, u32[]{:S(2)}, u32[]{:S(2)}) %collective-permute-start.5) | collective-permute-done | bytes 65568 | tf_op jit(solution)/shard_map/ppermute | solution.py:119
  67.9 5.8 %collective-permute-start.6 = (f32[128,128]{1,0:T(8,128)S(1)}, f32[128,128]{1,0:T(8,128)S(1)}, u32[]{:S(2)}, u32[]{:S(2)}) collective-permute-start(f32[128,128]{1,0:T(8,128)S(1)} %add.87), channel_id=1, source_target_pairs={{0,64},{16,80},{32,96},{48,112},{64,0},{80,16},{96,32},{112,48},{1... | collective-permute-start | bytes 196616 | tf_op jit(solution)/shard_map/ppermute | solution.py:119
  73.7 2.2 %collective-permute-start.14 = (f32[129,128]{1,0:T(8,128)S(1)}, f32[129,128]{1,0:T(8,128)S(1)}, u32[]{:S(2)}, u32[]{:S(2)}) collective-permute-start(f32[129,128]{1,0:T(8,128)S(1)} %add.96), channel_id=1, source_target_pairs={{0,64},{16,80},{32,96},{48,112},{64,0},{80,16},{96,32},{112,48},{1... | collective-permute-start | bytes 198152 | tf_op jit(solution)/shard_map/ppermute | solution.py:119
  75.9 0.5 collective-permute-done.6
  76.4 6.2 %collective-permute-start.7 = (f32[128,128]{1,0:T(8,128)S(1)}, f32[128,128]{1,0:T(8,128)S(1)}, u32[]{:S(2)}, u32[]{:S(2)}) collective-permute-start(f32[128,128]{1,0:T(8,128)S(1)} %add.88), channel_id=1, source_target_pairs={{0,128},{16,144},{32,160},{48,176},{64,192},{80,208},{96,224},{112... | collective-permute-start | bytes 196616 | tf_op jit(solution)/shard_map/ppermute | solution.py:119
  82.7 0.8 collective-permute-start.15
  83.5 1.9 %collective-permute-done.7 = f32[128,128]{1,0:T(8,128)S(1)} collective-permute-done((f32[128,128]{1,0:T(8,128)S(1)}, f32[128,128]{1,0:T(8,128)S(1)}, u32[]{:S(2)}, u32[]{:S(2)}) %collective-permute-start.7) | collective-permute-done | bytes 65568 | tf_op jit(solution)/shard_map/ppermute | solution.py:119
  85.5 5.8 %collective-permute-done.15 = f32[129,128]{1,0:T(8,128)S(1)} collective-permute-done((f32[129,128]{1,0:T(8,128)S(1)}, f32[129,128]{1,0:T(8,128)S(1)}, u32[]{:S(2)}, u32[]{:S(2)}) %collective-permute-start.15) | collective-permute-done | bytes 66080 | tf_op jit(solution)/shard_map/ppermute | solution.py:119
  91.5 4.2 %collective-permute-done.16 = f32[129,128]{1,0:T(8,128)S(1)} collective-permute-done((f32[129,128]{1,0:T(8,128)S(1)}, f32[129,128]{1,0:T(8,128)S(1)}, u32[]{:S(2)}, u32[]{:S(2)}) %collective-permute-start.16) | collective-permute-done | bytes 66080 | tf_op jit(solution)/shard_map/ppermute | solution.py:119
  95.7 0.3 collective-permute-start.17
  96.0 1.3 collective-permute-done.9
  97.3 1.6 collective-permute-start.10
  98.9 2.9 %collective-permute-done.17 = f32[129,128]{1,0:T(8,128)S(1)} collective-permute-done((f32[129,128]{1,0:T(8,128)S(1)}, f32[129,128]{1,0:T(8,128)S(1)}, u32[]{:S(2)}, u32[]{:S(2)}) %collective-permute-start.17) | collective-permute-done | bytes 66080 | tf_op jit(solution)/shard_map/ppermute | solution.py:119
  101.8 1.6 collective-permute-start.18
  103.4 1.6 collective-permute-start.11
  105.2 1.0 collective-permute-done.18
  106.2 3.3 %collective-permute-start.19 = (f32[129,128]{1,0:T(8,128)S(1)}, f32[129,128]{1,0:T(8,128)S(1)}, u32[]{:S(2)}, u32[]{:S(2)}) collective-permute-start(f32[129,128]{1,0:T(8,128)S(1)} %add.101), channel_id=1, source_target_pairs={{0,8},{1,9},{2,10},{3,11},{4,12},{5,13},{6,14},{7,15},{8,0},{9,1},... | collective-permute-start | bytes 198152 | tf_op jit(solution)/shard_map/ppermute | solution.py:119
  109.8 11.7 %cholesky.32 = f32[128,128]{1,0:T(8,128)S(1)} custom-call(f32[128,128]{1,0:T(8,128)S(1)} %fusion.34), custom_call_target="Cholesky" | custom-call | tf_op jit(solution)/shard_map/jit(cholesky)/cholesky | solution.py:173
  121.5 0.6 compare_reduce_fusion.1
  122.2 0.7 fusion.25
  122.9 9.8 %custom-call.12 = f32[1,128,128]{1,2,0:T(8,128)S(1)} custom-call(f32[1,128,128]{2,1,0:T(8,128)S(1)} %fusion.25), custom_call_target="InvertDiagBlocksLowerTriangular" | custom-call | tf_op jit(solution)/shard_map/triangular_solve | solution.py:125
  133.1 0.3 fusion.27
  133.6 0.3 slice_subtract_fusion
  134.0 11.6 %cholesky.67 = f32[127,127]{1,0:T(8,128)S(1)} custom-call(f32[127,127]{1,0:T(8,128)S(1)} %fusion.31), custom_call_target="Cholesky" | custom-call | tf_op jit(solution)/shard_map/jit(cholesky)/cholesky | solution.py:177
  145.7 0.6 compare_reduce_fusion
  146.3 0.7 fusion.26
  147.0 10.0 %custom-call.13 = f32[1,127,127]{1,2,0:T(8,128)S(1)} custom-call(f32[1,127,127]{2,1,0:T(8,128)S(1)} %fusion.26), custom_call_target="InvertDiagBlocksLowerTriangular" | custom-call | tf_op jit(solution)/shard_map/triangular_solve | solution.py:125
  157.0 0.3 fusion.29
  157.3 0.3 convolution_negate_fusion
  157.8 0.4 fusion.14
  158.2 1.1 fusion.23
  159.3 5.9 %fusion.4 = bf16[255,2,48,128]{3,0,2,1:T(8,128)(2,1)S(1)} fusion(bf16[256,2,48,128]{3,2,1,0:T(8,128)(2,1)} %shard_map.31, bf16[255,255]{1,0:T(8,128)(2,1)S(1)} %fusion.24), kind=kOutput, calls=%fused_computation.5 | convolution fusion | flops 1607454720 | bytes 12688386 | tf_op jit(solution)/shard_map/dot_general | solution.py:192
  165.2 6.7 %copy.28 = bf16[255,2,48,128]{3,2,1,0:T(8,128)(2,1)} copy(bf16[255,2,48,128]{3,0,2,1:T(8,128)(2,1)S(1)} %fusion.4) | data formatting | bytes 12533760
  (55 shorter events, 2.2 us)
Async XLA Ops:
  8.6 12.7 %collective-permute-start.3 = (f32[8,48,128]{2,1,0:T(8,128)}, f32[8,48,128]{2,1,0:T(8,128)S(1)}, u32[]{:S(2)}, u32[]{:S(2)}) collective-permute-start(f32[8,48,128]{2,1,0:T(8,128)} %shard_map.30), channel_id=1, source_target_pairs={{1,0},{2,1},{3,2},{4,3},{5,4},{6,5},{7,6},{8,7},{9,8},{10,9},{11,1... | collective-permute-start | bytes 589832 | tf_op jit(solution)/shard_map/ppermute | solution.py:149
  11.2 10.0 %collective-permute-start.2 = (f32[8,48,128]{2,1,0:T(8,128)}, f32[8,48,128]{2,1,0:T(8,128)S(1)}, u32[]{:S(2)}, u32[]{:S(2)}) collective-permute-start(f32[8,48,128]{2,1,0:T(8,128)} %shard_map.30), channel_id=1, source_target_pairs={{0,1},{1,2},{2,3},{3,4},{4,5},{5,6},{6,7},{7,8},{8,9},{9,10},{10,1... | collective-permute-start | bytes 589832 | tf_op jit(solution)/shard_map/ppermute | solution.py:148
  18.6 3.4 %collective-permute-start = (f32[256,2,128]{2,1,0:T(2,128)S(1)}, f32[256,2,128]{2,1,0:T(2,128)S(1)}, u32[]{:S(2)}, u32[]{:S(2)}) collective-permute-start(f32[256,2,128]{2,1,0:T(2,128)S(1)} %get-tuple-element.6), channel_id=1, source_target_pairs={{0,16},{16,32},{32,48},{48,64},{64,80},{80,96},{96,112},{112,128},... | collective-permute-start | bytes 786440 | tf_op jit(solution)/shard_map/ppermute | solution.py:138
  19.9 5.6 %collective-permute-start.1 = (f32[256,2,128]{2,1,0:T(2,128)S(1)}, f32[256,2,128]{2,1,0:T(2,128)S(1)}, u32[]{:S(2)}, u32[]{:S(2)}) collective-permute-start(f32[256,2,128]{2,1,0:T(2,128)S(1)} %get-tuple-element.7), channel_id=1, source_target_pairs={{16,0},{32,16},{48,32},{64,48},{80,64},{96,80},{112,96},{128,112},... | collective-permute-start | bytes 786440 | tf_op jit(solution)/shard_map/ppermute | solution.py:139
  57.4 8.1 %collective-permute-start.12 = (f32[129,128]{1,0:T(8,128)S(1)}, f32[129,128]{1,0:T(8,128)S(1)}, u32[]{:S(2)}, u32[]{:S(2)}) collective-permute-start(f32[129,128]{1,0:T(8,128)S(1)} %pad_maximum_fusion.4), channel_id=1, source_target_pairs={{0,16},{16,0},{32,48},{48,32},{64,80},{80,64},{96,112},{112,96},{1... | collective-permute-start | bytes 198152 | tf_op jit(solution)/shard_map/ppermute | solution.py:119
  62.2 1.3 collective-permute-start.4
  63.5 4.4 %collective-permute-start.5 = (f32[128,128]{1,0:T(8,128)S(1)}, f32[128,128]{1,0:T(8,128)S(1)}, u32[]{:S(2)}, u32[]{:S(2)}) collective-permute-start(f32[128,128]{1,0:T(8,128)S(1)} %add.86), channel_id=1, source_target_pairs={{0,32},{16,48},{32,0},{48,16},{64,96},{80,112},{96,64},{112,80},{1... | collective-permute-start | bytes 196616 | tf_op jit(solution)/shard_map/ppermute | solution.py:119
  65.5 8.2 %collective-permute-start.13 = (f32[129,128]{1,0:T(8,128)S(1)}, f32[129,128]{1,0:T(8,128)S(1)}, u32[]{:S(2)}, u32[]{:S(2)}) collective-permute-start(f32[129,128]{1,0:T(8,128)S(1)} %fusion.42), channel_id=1, source_target_pairs={{0,32},{16,48},{32,0},{48,16},{64,96},{80,112},{96,64},{112,80},{1... | collective-permute-start | bytes 198152 | tf_op jit(solution)/shard_map/ppermute | solution.py:119
  67.9 8.5 %collective-permute-start.6 = (f32[128,128]{1,0:T(8,128)S(1)}, f32[128,128]{1,0:T(8,128)S(1)}, u32[]{:S(2)}, u32[]{:S(2)}) collective-permute-start(f32[128,128]{1,0:T(8,128)S(1)} %add.87), channel_id=1, source_target_pairs={{0,64},{16,80},{32,96},{48,112},{64,0},{80,16},{96,32},{112,48},{1... | collective-permute-start | bytes 196616 | tf_op jit(solution)/shard_map/ppermute | solution.py:119
  73.7 8.9 %collective-permute-start.14 = (f32[129,128]{1,0:T(8,128)S(1)}, f32[129,128]{1,0:T(8,128)S(1)}, u32[]{:S(2)}, u32[]{:S(2)}) collective-permute-start(f32[129,128]{1,0:T(8,128)S(1)} %add.96), channel_id=1, source_target_pairs={{0,64},{16,80},{32,96},{48,112},{64,0},{80,16},{96,32},{112,48},{1... | collective-permute-start | bytes 198152 | tf_op jit(solution)/shard_map/ppermute | solution.py:119
  76.4 8.9 %collective-permute-start.7 = (f32[128,128]{1,0:T(8,128)S(1)}, f32[128,128]{1,0:T(8,128)S(1)}, u32[]{:S(2)}, u32[]{:S(2)}) collective-permute-start(f32[128,128]{1,0:T(8,128)S(1)} %add.88), channel_id=1, source_target_pairs={{0,128},{16,144},{32,160},{48,176},{64,192},{80,208},{96,224},{112... | collective-permute-start | bytes 196616 | tf_op jit(solution)/shard_map/ppermute | solution.py:119
  82.7 8.6 %collective-permute-start.15 = (f32[129,128]{1,0:T(8,128)S(1)}, f32[129,128]{1,0:T(8,128)S(1)}, u32[]{:S(2)}, u32[]{:S(2)}) collective-permute-start(f32[129,128]{1,0:T(8,128)S(1)} %add.97), channel_id=1, source_target_pairs={{0,128},{16,144},{32,160},{48,176},{64,192},{80,208},{96,224},{112... | collective-permute-start | bytes 198152 | tf_op jit(solution)/shard_map/ppermute | solution.py:119
  85.4 6.0 %collective-permute-start.8 = (f32[128,128]{1,0:T(8,128)S(1)}, f32[128,128]{1,0:T(8,128)S(1)}, u32[]{:S(2)}, u32[]{:S(2)}) collective-permute-start(f32[128,128]{1,0:T(8,128)S(1)} %add.89), channel_id=1, source_target_pairs={{0,1},{1,0},{2,3},{3,2},{4,5},{5,4},{6,7},{7,6},{8,9},{9,8},{10,11... | collective-permute-start | bytes 196616 | tf_op jit(solution)/shard_map/ppermute | solution.py:119
  91.3 4.4 %collective-permute-start.16 = (f32[129,128]{1,0:T(8,128)S(1)}, f32[129,128]{1,0:T(8,128)S(1)}, u32[]{:S(2)}, u32[]{:S(2)}) collective-permute-start(f32[129,128]{1,0:T(8,128)S(1)} %add.98), channel_id=1, source_target_pairs={{0,1},{1,0},{2,3},{3,2},{4,5},{5,4},{6,7},{7,6},{8,9},{9,8},{10,11... | collective-permute-start | bytes 198152 | tf_op jit(solution)/shard_map/ppermute | solution.py:119
  91.4 5.9 %collective-permute-start.9 = (f32[128,128]{1,0:T(8,128)S(1)}, f32[128,128]{1,0:T(8,128)S(1)}, u32[]{:S(2)}, u32[]{:S(2)}) collective-permute-start(f32[128,128]{1,0:T(8,128)S(1)} %add.90), channel_id=1, source_target_pairs={{0,2},{1,3},{2,0},{3,1},{4,6},{5,7},{6,4},{7,5},{8,10},{9,11},{10,... | collective-permute-start | bytes 196616 | tf_op jit(solution)/shard_map/ppermute | solution.py:119
  95.7 6.1 %collective-permute-start.17 = (f32[129,128]{1,0:T(8,128)S(1)}, f32[129,128]{1,0:T(8,128)S(1)}, u32[]{:S(2)}, u32[]{:S(2)}) collective-permute-start(f32[129,128]{1,0:T(8,128)S(1)} %add.99), channel_id=1, source_target_pairs={{0,2},{1,3},{2,0},{3,1},{4,6},{5,7},{6,4},{7,5},{8,10},{9,11},{10,... | collective-permute-start | bytes 198152 | tf_op jit(solution)/shard_map/ppermute | solution.py:119
  97.3 6.1 %collective-permute-start.10 = (f32[128,128]{1,0:T(8,128)S(1)}, f32[128,128]{1,0:T(8,128)S(1)}, u32[]{:S(2)}, u32[]{:S(2)}) collective-permute-start(f32[128,128]{1,0:T(8,128)S(1)} %add.91), channel_id=1, source_target_pairs={{0,4},{1,5},{2,6},{3,7},{4,0},{5,1},{6,2},{7,3},{8,12},{9,13},{10,... | collective-permute-start | bytes 196616 | tf_op jit(solution)/shard_map/ppermute | solution.py:119
  101.8 4.4 %collective-permute-start.18 = (f32[129,128]{1,0:T(8,128)S(1)}, f32[129,128]{1,0:T(8,128)S(1)}, u32[]{:S(2)}, u32[]{:S(2)}) collective-permute-start(f32[129,128]{1,0:T(8,128)S(1)} %add.100), channel_id=1, source_target_pairs={{0,4},{1,5},{2,6},{3,7},{4,0},{5,1},{6,2},{7,3},{8,12},{9,13},{10,... | collective-permute-start | bytes 198152 | tf_op jit(solution)/shard_map/ppermute | solution.py:119
  103.4 6.1 %collective-permute-start.11 = (f32[128,128]{1,0:T(8,128)S(1)}, f32[128,128]{1,0:T(8,128)S(1)}, u32[]{:S(2)}, u32[]{:S(2)}) collective-permute-start(f32[128,128]{1,0:T(8,128)S(1)} %add.92), channel_id=1, source_target_pairs={{0,8},{1,9},{2,10},{3,11},{4,12},{5,13},{6,14},{7,15},{8,0},{9,1},... | collective-permute-start | bytes 196616 | tf_op jit(solution)/shard_map/ppermute | solution.py:119
  106.2 26.8 %collective-permute-start.19 = (f32[129,128]{1,0:T(8,128)S(1)}, f32[129,128]{1,0:T(8,128)S(1)}, u32[]{:S(2)}, u32[]{:S(2)}) collective-permute-start(f32[129,128]{1,0:T(8,128)S(1)} %add.101), channel_id=1, source_target_pairs={{0,8},{1,9},{2,10},{3,11},{4,12},{5,13},{6,14},{7,15},{8,0},{9,1},... | collective-permute-start | bytes 198152 | tf_op jit(solution)/shard_map/ppermute | solution.py:119

commit v3 on v2

--- a/solution.py
+++ b/solution.py
@@ -112,10 +112,10 @@
     )
 
 
-def doubling_sum(value, axis):
+def doubling_sum(value, axis, step=1, stop=None):
     count = lax.axis_size(axis)
-    step = 1
-    while step < count:
+    stop = count if stop is None else stop
+    while step < stop:
         value = value + lax.ppermute(value, axis, [(i, i ^ step) for i in range(count)])
         step *= 2
     return value
@@ -161,8 +161,10 @@
     )
     half = snaps // 2
     packed = pack_symmetric(local_gram)
-    folded = doubling_sum(doubling_sum(packed[half : 2 * half], "gx"), "gy")
+    folded = doubling_sum(packed[half : 2 * half], "gx", 1, 4)
     edge = jnp.concatenate([packed[:half], packed[2 * half :]], axis=0)
+    folded, edge = lax.optimization_barrier((folded, edge))
+    folded = doubling_sum(doubling_sum(folded, "gx", 4), "gy")
     edge = doubling_sum(doubling_sum(edge, "gx"), "gy")
     side = edge[:half]
     gram = unpack_symmetric(jnp.concatenate([side, folded, edge[half:]], axis=0))

time: 172 us -> 177 us (1.029)
  starting transfers between devices: 41.4 us -> 47.9 us
  waiting for transfers between devices: 24.5 us -> 21.3 us
    ppermute x16, starting transfers between devices: 30.8 us -> 37.3 us  [doubling_sum(): lax.ppermute(value, axis, [(i, i ^ step) for i in range(count)])]
    ppermute x16, waiting for transfers between devices: 21 us -> 17.8 us  [doubling_sum(): lax.ppermute(value, axis, [(i, i ^ step) for i in range(count)])]
  transfers between devices with their start and end apart: 20 -> 20, of which waited for: 10 -> 11; matrix products, arithmetic and copies ran while one was open for 15% -> 16% of each run, Pallas kernels for 0% -> 0%
where the time goes in v3:
time: 177 us; the launch traced here: 175 us
  other arithmetic  49.7 us (28%)
  starting transfers between devices  47.9 us (27%)
  Pallas kernels  29.5 us (17%)
  waiting for transfers between devices  21.3 us (12%)
  matrix products  17 us (10%)
  local copies, waits for them, and re-layouts  8.94 us (5%)
    ppermute x16, starting transfers between devices, doubling_sum(): lax.ppermute(value, axis, [(i, i ^ step) for i in range(count)])  37.3 us
    pallas_call x1, Pallas kernels, features_of(): pl.pallas_call(feature_kernel, grid=(snaps // block,), in_specs=[pl.Block...  21.6 us
    another operation x4, other arithmetic, tri_solve(): return lax.linalg.triangular_solve(lower, right, left_side=True, lower=True)  20.9 us
    ppermute x16, waiting for transfers between devices, doubling_sum(): lax.ppermute(value, axis, [(i, i ^ step) for i in range(count)])  17.8 us
    another operation x4, other arithmetic, shards(): low11 = jnp.linalg.cholesky(lead)  12.4 us
    another operation x3, other arithmetic, shards(): low22 = jnp.linalg.cholesky(schur)  12.3 us
    dot_general x1, matrix products, shards(): lax.dot_general(features, features, (((1, 2, 3), (1, 2, 3)), ((), ())), p...  7.98 us
    pallas_call x1, Pallas kernels, edges_of(): pl.pallas_call(edge_kernel, grid=(snaps // block,), in_specs=[pl.BlockSpe...  7.92 us
  transfers between devices with their start and end apart: 20, of which 11 were waited for; matrix products, arithmetic and copies ran while one was open for 16% of the time, Pallas kernels for 0%

profile of v3, /device:TPU:24, one launch (start us, length us, event | category | flops | bytes accessed | tf_op | source)
XLA Modules:
  0.0 175.3 jit_solution(14800740591264477777)
XLA Ops:
  0.6 7.9 %shard_map.30 = f32[8,48,128]{2,1,0:T(8,128)} custom-call(bf16[2,256,48,128]{3,2,1,0:T(8,128)(2,1)} %ener_ref.3, bf16[2,256,48,128]{3,2,1,0:T(8,128)(2,1)} %ener_ref.3), custom_call_target="tpu_custom_call" | custom-call | tf_op jit(solution)/shard_map/pallas_call | solution.py:72
  8.6 2.6 %collective-permute-start.3 = (f32[8,48,128]{2,1,0:T(8,128)}, f32[8,48,128]{2,1,0:T(8,128)S(1)}, u32[]{:S(2)}, u32[]{:S(2)}) collective-permute-start(f32[8,48,128]{2,1,0:T(8,128)} %shard_map.30), channel_id=1, source_target_pairs={{1,0},{2,1},{3,2},{4,3},{5,4},{6,5},{7,6},{8,7},{9,8},{10,9},{11,1... | collective-permute-start | bytes 589832 | tf_op jit(solution)/shard_map/ppermute | solution.py:149
  11.2 5.3 %collective-permute-start.2 = (f32[8,48,128]{2,1,0:T(8,128)}, f32[8,48,128]{2,1,0:T(8,128)S(1)}, u32[]{:S(2)}, u32[]{:S(2)}) collective-permute-start(f32[8,48,128]{2,1,0:T(8,128)} %shard_map.30), channel_id=1, source_target_pairs={{0,1},{1,2},{2,3},{3,4},{4,5},{5,6},{6,7},{7,8},{8,9},{9,10},{10,1... | collective-permute-start | bytes 589832 | tf_op jit(solution)/shard_map/ppermute | solution.py:148
  16.5 2.0 %fusion.19 = (f32[256,2,128]{2,1,0:T(2,128)S(1)}, f32[256,2,128]{2,1,0:T(2,128)S(1)}) fusion(bf16[2,256,48,128]{3,2,1,0:T(8,128)(2,1)} %ener_ref.3), kind=kLoop, calls=%fused_computation.21 | loop fusion | flops 524288 | bytes 1048576 | tf_op jit(solution)/shard_map/div | solution.py:134
  18.6 1.3 collective-permute-start
  19.9 1.3 collective-permute-start.1
  21.2 0.7 fusion.20.yh_ref
  21.9 3.5 %collective-permute-done.1 = f32[256,2,128]{2,1,0:T(2,128)S(1)} collective-permute-done((f32[256,2,128]{2,1,0:T(2,128)S(1)}, f32[256,2,128]{2,1,0:T(2,128)S(1)}, u32[]{:S(2)}, u32[]{:S(2)}) %collective-permute-start.1) | collective-permute-done | bytes 262176 | tf_op jit(solution)/shard_map/ppermute | solution.py:139
  25.4 1.0 pad_maximum_fusion.xh_ref
  26.5 21.6 %shard_map.31 = bf16[256,2,48,128]{3,2,1,0:T(8,128)(2,1)} custom-call(bf16[2,256,48,128]{3,2,1,0:T(8,128)(2,1)} %ener_ref.3, bf16[2,256,48,128]{3,2,1,0:T(8,128)(2,1)} %ener_ref.3, f32[256,4,128]{2,1,0:T(4,128)} %pad_maximum_fusion.xh_ref, f32[8,48,128]{2,1,0:T(8,128)} %fusion.20.yh_ref), custom_call_target="tpu_custom_call" | custom-call | tf_op jit(solution)/shard_map/pallas_call | solution.py:43
  48.1 8.0 %fusion.10 = f32[256,256]{1,0:T(8,128)S(1)} fusion(bf16[256,2,48,128]{3,2,1,0:T(8,128)(2,1)} %shard_map.31), kind=kOutput, calls=%fused_computation.7 | convolution fusion | flops 1610678272 | bytes 6553600 | tf_op jit(solution)/shard_map/dot_general | solution.py:157
  56.1 4.8 %collective-permute-start.4 = (f32[128,128]{1,0:T(8,128)S(1)}, f32[128,128]{1,0:T(8,128)S(1)}, u32[]{:S(2)}, u32[]{:S(2)}) collective-permute-start(f32[128,128]{1,0:T(8,128)S(1)} %get-tuple-element.14), channel_id=1, source_target_pairs={{0,16},{16,0},{32,48},{48,32},{64,80},{80,64},{96,112},{112,96},{1... | collective-permute-start | bytes 196616 | tf_op jit(solution)/shard_map/ppermute | solution.py:119
  61.0 1.2 gather_fusion
  62.2 2.0 %collective-permute-start.5 = (f32[128,128]{1,0:T(8,128)S(1)}, f32[128,128]{1,0:T(8,128)S(1)}, u32[]{:S(2)}, u32[]{:S(2)}) collective-permute-start(f32[128,128]{1,0:T(8,128)S(1)} %add.86), channel_id=1, source_target_pairs={{0,32},{16,48},{32,0},{48,16},{64,96},{80,112},{96,64},{112,80},{1... | collective-permute-start | bytes 196616 | tf_op jit(solution)/shard_map/ppermute | solution.py:119
  64.2 2.3 %collective-permute-done.5 = f32[128,128]{1,0:T(8,128)S(1)} collective-permute-done((f32[128,128]{1,0:T(8,128)S(1)}, f32[128,128]{1,0:T(8,128)S(1)}, u32[]{:S(2)}, u32[]{:S(2)}) %collective-permute-start.5) | collective-permute-done | bytes 65568 | tf_op jit(solution)/shard_map/ppermute | solution.py:119
  66.6 5.7 %collective-permute-start.6 = (f32[128,128]{1,0:T(8,128)S(1)}, f32[128,128]{1,0:T(8,128)S(1)}, u32[]{:S(2)}, u32[]{:S(2)}) collective-permute-start(f32[128,128]{1,0:T(8,128)S(1)} %add.87), channel_id=1, source_target_pairs={{0,64},{16,80},{32,96},{48,112},{64,0},{80,16},{96,32},{112,48},{1... | collective-permute-start | bytes 196616 | tf_op jit(solution)/shard_map/ppermute | solution.py:119
  72.3 2.5 %collective-permute-done.6 = f32[128,128]{1,0:T(8,128)S(1)} collective-permute-done((f32[128,128]{1,0:T(8,128)S(1)}, f32[128,128]{1,0:T(8,128)S(1)}, u32[]{:S(2)}, u32[]{:S(2)}) %collective-permute-start.6) | collective-permute-done | bytes 65568 | tf_op jit(solution)/shard_map/ppermute | solution.py:119
  74.9 4.2 %collective-permute-start.7 = (f32[128,128]{1,0:T(8,128)S(1)}, f32[128,128]{1,0:T(8,128)S(1)}, u32[]{:S(2)}, u32[]{:S(2)}) collective-permute-start(f32[128,128]{1,0:T(8,128)S(1)} %add.88), channel_id=1, source_target_pairs={{0,128},{16,144},{32,160},{48,176},{64,192},{80,208},{96,224},{112... | collective-permute-start | bytes 196616 | tf_op jit(solution)/shard_map/ppermute | solution.py:119
  79.1 0.3 collective-permute-start.13
  79.5 3.8 %collective-permute-done.7 = f32[128,128]{1,0:T(8,128)S(1)} collective-permute-done((f32[128,128]{1,0:T(8,128)S(1)}, f32[128,128]{1,0:T(8,128)S(1)}, u32[]{:S(2)}, u32[]{:S(2)}) %collective-permute-start.7) | collective-permute-done | bytes 65568 | tf_op jit(solution)/shard_map/ppermute | solution.py:119
  83.5 3.1 %collective-permute-start.14 = (f32[129,128]{1,0:T(8,128)S(1)}, f32[129,128]{1,0:T(8,128)S(1)}, u32[]{:S(2)}, u32[]{:S(2)}) collective-permute-start(f32[129,128]{1,0:T(8,128)S(1)} %add.96), channel_id=1, source_target_pairs={{0,64},{16,80},{32,96},{48,112},{64,0},{80,16},{96,32},{112,48},{1... | collective-permute-start | bytes 198152 | tf_op jit(solution)/shard_map/ppermute | solution.py:119
  86.7 0.9 collective-permute-done.8
  87.7 1.2 collective-permute-done.14
  89.0 4.4 %collective-permute-start.15 = (f32[129,128]{1,0:T(8,128)S(1)}, f32[129,128]{1,0:T(8,128)S(1)}, u32[]{:S(2)}, u32[]{:S(2)}) collective-permute-start(f32[129,128]{1,0:T(8,128)S(1)} %add.97), channel_id=1, source_target_pairs={{0,128},{16,144},{32,160},{48,176},{64,192},{80,208},{96,224},{112... | collective-permute-start | bytes 198152 | tf_op jit(solution)/shard_map/ppermute | solution.py:119
  93.5 1.6 collective-permute-start.10
  95.1 2.2 %collective-permute-done.15 = f32[129,128]{1,0:T(8,128)S(1)} collective-permute-done((f32[129,128]{1,0:T(8,128)S(1)}, f32[129,128]{1,0:T(8,128)S(1)}, u32[]{:S(2)}, u32[]{:S(2)}) %collective-permute-start.15) | collective-permute-done | bytes 66080 | tf_op jit(solution)/shard_map/ppermute | solution.py:119
  97.3 2.3 %collective-permute-start.16 = (f32[129,128]{1,0:T(8,128)S(1)}, f32[129,128]{1,0:T(8,128)S(1)}, u32[]{:S(2)}, u32[]{:S(2)}) collective-permute-start(f32[129,128]{1,0:T(8,128)S(1)} %add.98), channel_id=1, source_target_pairs={{0,1},{1,0},{2,3},{3,2},{4,5},{5,4},{6,7},{7,6},{8,9},{9,8},{10,11... | collective-permute-start | bytes 198152 | tf_op jit(solution)/shard_map/ppermute | solution.py:119
  99.6 3.1 %collective-permute-start.11 = (f32[128,128]{1,0:T(8,128)S(1)}, f32[128,128]{1,0:T(8,128)S(1)}, u32[]{:S(2)}, u32[]{:S(2)}) collective-permute-start(f32[128,128]{1,0:T(8,128)S(1)} %add.92), channel_id=1, source_target_pairs={{0,8},{1,9},{2,10},{3,11},{4,12},{5,13},{6,14},{7,15},{8,0},{9,1},... | collective-permute-start | bytes 196616 | tf_op jit(solution)/shard_map/ppermute | solution.py:119
  102.9 2.1 %collective-permute-start.17 = (f32[129,128]{1,0:T(8,128)S(1)}, f32[129,128]{1,0:T(8,128)S(1)}, u32[]{:S(2)}, u32[]{:S(2)}) collective-permute-start(f32[129,128]{1,0:T(8,128)S(1)} %add.99), channel_id=1, source_target_pairs={{0,2},{1,3},{2,0},{3,1},{4,6},{5,7},{6,4},{7,5},{8,10},{9,11},{10,... | collective-permute-start | bytes 198152 | tf_op jit(solution)/shard_map/ppermute | solution.py:119
  105.0 0.5 collective-permute-done.11
  105.7 11.7 %cholesky.32 = f32[128,128]{1,0:T(8,128)S(1)} custom-call(f32[128,128]{1,0:T(8,128)S(1)} %fusion.34), custom_call_target="Cholesky" | custom-call | tf_op jit(solution)/shard_map/jit(cholesky)/cholesky | solution.py:175
  117.5 0.6 compare_reduce_fusion.1
  118.1 1.6 collective-permute-start.18
  119.7 0.7 fusion.25
  120.4 9.8 %custom-call.12 = f32[1,128,128]{1,2,0:T(8,128)S(1)} custom-call(f32[1,128,128]{2,1,0:T(8,128)S(1)} %fusion.25), custom_call_target="InvertDiagBlocksLowerTriangular" | custom-call | tf_op jit(solution)/shard_map/triangular_solve | solution.py:125
  130.2 1.9 %collective-permute-start.19 = (f32[129,128]{1,0:T(8,128)S(1)}, f32[129,128]{1,0:T(8,128)S(1)}, u32[]{:S(2)}, u32[]{:S(2)}) collective-permute-start(f32[129,128]{1,0:T(8,128)S(1)} %add.101), channel_id=1, source_target_pairs={{0,8},{1,9},{2,10},{3,11},{4,12},{5,13},{6,14},{7,15},{8,0},{9,1},... | collective-permute-start | bytes 198152 | tf_op jit(solution)/shard_map/ppermute | solution.py:119
  132.4 3.9 %collective-permute-done.19 = f32[129,128]{1,0:T(8,128)S(1)} collective-permute-done((f32[129,128]{1,0:T(8,128)S(1)}, f32[129,128]{1,0:T(8,128)S(1)}, u32[]{:S(2)}, u32[]{:S(2)}) %collective-permute-start.19) | collective-permute-done | bytes 66080 | tf_op jit(solution)/shard_map/ppermute | solution.py:119
  136.4 0.3 fusion.27
  136.9 0.3 slice_subtract_fusion
  137.3 11.6 %cholesky.67 = f32[127,127]{1,0:T(8,128)S(1)} custom-call(f32[127,127]{1,0:T(8,128)S(1)} %fusion.31), custom_call_target="Cholesky" | custom-call | tf_op jit(solution)/shard_map/jit(cholesky)/cholesky | solution.py:179
  149.0 0.6 compare_reduce_fusion
  149.6 0.7 fusion.26
  150.3 9.7 %custom-call.13 = f32[1,127,127]{1,2,0:T(8,128)S(1)} custom-call(f32[1,127,127]{2,1,0:T(8,128)S(1)} %fusion.26), custom_call_target="InvertDiagBlocksLowerTriangular" | custom-call | tf_op jit(solution)/shard_map/triangular_solve | solution.py:125
  160.4 0.3 convolution_negate_fusion
  160.8 0.4 fusion.14
  161.3 1.1 fusion.23
  162.4 5.9 %fusion.4 = bf16[255,2,48,128]{3,0,2,1:T(8,128)(2,1)S(1)} fusion(bf16[256,2,48,128]{3,2,1,0:T(8,128)(2,1)} %shard_map.31, bf16[255,255]{1,0:T(8,128)(2,1)S(1)} %fusion.24), kind=kOutput, calls=%fused_computation.5 | convolution fusion | flops 1607454720 | bytes 12688386 | tf_op jit(solution)/shard_map/dot_general | solution.py:194
  168.3 7.0 %copy.28 = bf16[255,2,48,128]{3,2,1,0:T(8,128)(2,1)} copy(bf16[255,2,48,128]{3,0,2,1:T(8,128)(2,1)S(1)} %fusion.4) | data formatting | bytes 12533760
  (55 shorter events, 2.4 us)
Async XLA Ops:
  8.6 12.6 %collective-permute-start.3 = (f32[8,48,128]{2,1,0:T(8,128)}, f32[8,48,128]{2,1,0:T(8,128)S(1)}, u32[]{:S(2)}, u32[]{:S(2)}) collective-permute-start(f32[8,48,128]{2,1,0:T(8,128)} %shard_map.30), channel_id=1, source_target_pairs={{1,0},{2,1},{3,2},{4,3},{5,4},{6,5},{7,6},{8,7},{9,8},{10,9},{11,1... | collective-permute-start | bytes 589832 | tf_op jit(solution)/shard_map/ppermute | solution.py:149
  11.2 10.0 %collective-permute-start.2 = (f32[8,48,128]{2,1,0:T(8,128)}, f32[8,48,128]{2,1,0:T(8,128)S(1)}, u32[]{:S(2)}, u32[]{:S(2)}) collective-permute-start(f32[8,48,128]{2,1,0:T(8,128)} %shard_map.30), channel_id=1, source_target_pairs={{0,1},{1,2},{2,3},{3,4},{4,5},{5,6},{6,7},{7,8},{8,9},{9,10},{10,1... | collective-permute-start | bytes 589832 | tf_op jit(solution)/shard_map/ppermute | solution.py:148
  18.6 3.4 %collective-permute-start = (f32[256,2,128]{2,1,0:T(2,128)S(1)}, f32[256,2,128]{2,1,0:T(2,128)S(1)}, u32[]{:S(2)}, u32[]{:S(2)}) collective-permute-start(f32[256,2,128]{2,1,0:T(2,128)S(1)} %get-tuple-element.10), channel_id=1, source_target_pairs={{0,16},{16,32},{32,48},{48,64},{64,80},{80,96},{96,112},{112,128},... | collective-permute-start | bytes 786440 | tf_op jit(solution)/shard_map/ppermute | solution.py:138
  19.9 5.6 %collective-permute-start.1 = (f32[256,2,128]{2,1,0:T(2,128)S(1)}, f32[256,2,128]{2,1,0:T(2,128)S(1)}, u32[]{:S(2)}, u32[]{:S(2)}) collective-permute-start(f32[256,2,128]{2,1,0:T(2,128)S(1)} %get-tuple-element.11), channel_id=1, source_target_pairs={{16,0},{32,16},{48,32},{64,48},{80,64},{96,80},{112,96},{128,112},... | collective-permute-start | bytes 786440 | tf_op jit(solution)/shard_map/ppermute | solution.py:139
  56.1 6.1 %collective-permute-start.4 = (f32[128,128]{1,0:T(8,128)S(1)}, f32[128,128]{1,0:T(8,128)S(1)}, u32[]{:S(2)}, u32[]{:S(2)}) collective-permute-start(f32[128,128]{1,0:T(8,128)S(1)} %get-tuple-element.14), channel_id=1, source_target_pairs={{0,16},{16,0},{32,48},{48,32},{64,80},{80,64},{96,112},{112,96},{1... | collective-permute-start | bytes 196616 | tf_op jit(solution)/shard_map/ppermute | solution.py:119
  62.2 4.4 %collective-permute-start.5 = (f32[128,128]{1,0:T(8,128)S(1)}, f32[128,128]{1,0:T(8,128)S(1)}, u32[]{:S(2)}, u32[]{:S(2)}) collective-permute-start(f32[128,128]{1,0:T(8,128)S(1)} %add.86), channel_id=1, source_target_pairs={{0,32},{16,48},{32,0},{48,16},{64,96},{80,112},{96,64},{112,80},{1... | collective-permute-start | bytes 196616 | tf_op jit(solution)/shard_map/ppermute | solution.py:119
  66.6 8.3 %collective-permute-start.6 = (f32[128,128]{1,0:T(8,128)S(1)}, f32[128,128]{1,0:T(8,128)S(1)}, u32[]{:S(2)}, u32[]{:S(2)}) collective-permute-start(f32[128,128]{1,0:T(8,128)S(1)} %add.87), channel_id=1, source_target_pairs={{0,64},{16,80},{32,96},{48,112},{64,0},{80,16},{96,32},{112,48},{1... | collective-permute-start | bytes 196616 | tf_op jit(solution)/shard_map/ppermute | solution.py:119
  72.3 6.8 %collective-permute-start.12 = (f32[129,128]{1,0:T(8,128)S(1)}, f32[129,128]{1,0:T(8,128)S(1)}, u32[]{:S(2)}, u32[]{:S(2)}) collective-permute-start(f32[129,128]{1,0:T(8,128)S(1)} %pad_maximum_fusion.4), channel_id=1, source_target_pairs={{0,16},{16,0},{32,48},{48,32},{64,80},{80,64},{96,112},{112,96},{1... | collective-permute-start | bytes 198152 | tf_op jit(solution)/shard_map/ppermute | solution.py:119
  74.9 8.4 %collective-permute-start.7 = (f32[128,128]{1,0:T(8,128)S(1)}, f32[128,128]{1,0:T(8,128)S(1)}, u32[]{:S(2)}, u32[]{:S(2)}) collective-permute-start(f32[128,128]{1,0:T(8,128)S(1)} %add.88), channel_id=1, source_target_pairs={{0,128},{16,144},{32,160},{48,176},{64,192},{80,208},{96,224},{112... | collective-permute-start | bytes 196616 | tf_op jit(solution)/shard_map/ppermute | solution.py:119
  79.1 4.4 %collective-permute-start.13 = (f32[129,128]{1,0:T(8,128)S(1)}, f32[129,128]{1,0:T(8,128)S(1)}, u32[]{:S(2)}, u32[]{:S(2)}) collective-permute-start(f32[129,128]{1,0:T(8,128)S(1)} %add.95), channel_id=1, source_target_pairs={{0,32},{16,48},{32,0},{48,16},{64,96},{80,112},{96,64},{112,80},{1... | collective-permute-start | bytes 198152 | tf_op jit(solution)/shard_map/ppermute | solution.py:119
  83.3 4.4 %collective-permute-start.8 = (f32[128,128]{1,0:T(8,128)S(1)}, f32[128,128]{1,0:T(8,128)S(1)}, u32[]{:S(2)}, u32[]{:S(2)}) collective-permute-start(f32[128,128]{1,0:T(8,128)S(1)} %add.89), channel_id=1, source_target_pairs={{0,1},{1,0},{2,3},{3,2},{4,5},{5,4},{6,7},{7,6},{8,9},{9,8},{10,11... | collective-permute-start | bytes 196616 | tf_op jit(solution)/shard_map/ppermute | solution.py:119
  83.5 5.4 %collective-permute-start.14 = (f32[129,128]{1,0:T(8,128)S(1)}, f32[129,128]{1,0:T(8,128)S(1)}, u32[]{:S(2)}, u32[]{:S(2)}) collective-permute-start(f32[129,128]{1,0:T(8,128)S(1)} %add.96), channel_id=1, source_target_pairs={{0,64},{16,80},{32,96},{48,112},{64,0},{80,16},{96,32},{112,48},{1... | collective-permute-start | bytes 198152 | tf_op jit(solution)/shard_map/ppermute | solution.py:119
  87.6 5.9 %collective-permute-start.9 = (f32[128,128]{1,0:T(8,128)S(1)}, f32[128,128]{1,0:T(8,128)S(1)}, u32[]{:S(2)}, u32[]{:S(2)}) collective-permute-start(f32[128,128]{1,0:T(8,128)S(1)} %add.90), channel_id=1, source_target_pairs={{0,2},{1,3},{2,0},{3,1},{4,6},{5,7},{6,4},{7,5},{8,10},{9,11},{10,... | collective-permute-start | bytes 196616 | tf_op jit(solution)/shard_map/ppermute | solution.py:119
  89.0 8.3 %collective-permute-start.15 = (f32[129,128]{1,0:T(8,128)S(1)}, f32[129,128]{1,0:T(8,128)S(1)}, u32[]{:S(2)}, u32[]{:S(2)}) collective-permute-start(f32[129,128]{1,0:T(8,128)S(1)} %add.97), channel_id=1, source_target_pairs={{0,128},{16,144},{32,160},{48,176},{64,192},{80,208},{96,224},{112... | collective-permute-start | bytes 198152 | tf_op jit(solution)/shard_map/ppermute | solution.py:119
  93.5 6.1 %collective-permute-start.10 = (f32[128,128]{1,0:T(8,128)S(1)}, f32[128,128]{1,0:T(8,128)S(1)}, u32[]{:S(2)}, u32[]{:S(2)}) collective-permute-start(f32[128,128]{1,0:T(8,128)S(1)} %add.91), channel_id=1, source_target_pairs={{0,4},{1,5},{2,6},{3,7},{4,0},{5,1},{6,2},{7,3},{8,12},{9,13},{10,... | collective-permute-start | bytes 196616 | tf_op jit(solution)/shard_map/ppermute | solution.py:119
  97.3 5.6 %collective-permute-start.16 = (f32[129,128]{1,0:T(8,128)S(1)}, f32[129,128]{1,0:T(8,128)S(1)}, u32[]{:S(2)}, u32[]{:S(2)}) collective-permute-start(f32[129,128]{1,0:T(8,128)S(1)} %add.98), channel_id=1, source_target_pairs={{0,1},{1,0},{2,3},{3,2},{4,5},{5,4},{6,7},{7,6},{8,9},{9,8},{10,11... | collective-permute-start | bytes 198152 | tf_op jit(solution)/shard_map/ppermute | solution.py:119
  99.6 5.9 %collective-permute-start.11 = (f32[128,128]{1,0:T(8,128)S(1)}, f32[128,128]{1,0:T(8,128)S(1)}, u32[]{:S(2)}, u32[]{:S(2)}) collective-permute-start(f32[128,128]{1,0:T(8,128)S(1)} %add.92), channel_id=1, source_target_pairs={{0,8},{1,9},{2,10},{3,11},{4,12},{5,13},{6,14},{7,15},{8,0},{9,1},... | collective-permute-start | bytes 196616 | tf_op jit(solution)/shard_map/ppermute | solution.py:119
  102.9 15.2 %collective-permute-start.17 = (f32[129,128]{1,0:T(8,128)S(1)}, f32[129,128]{1,0:T(8,128)S(1)}, u32[]{:S(2)}, u32[]{:S(2)}) collective-permute-start(f32[129,128]{1,0:T(8,128)S(1)} %add.99), channel_id=1, source_target_pairs={{0,2},{1,3},{2,0},{3,1},{4,6},{5,7},{6,4},{7,5},{8,10},{9,11},{10,... | collective-permute-start | bytes 198152 | tf_op jit(solution)/shard_map/ppermute | solution.py:119
  118.1 12.1 %collective-permute-start.18 = (f32[129,128]{1,0:T(8,128)S(1)}, f32[129,128]{1,0:T(8,128)S(1)}, u32[]{:S(2)}, u32[]{:S(2)}) collective-permute-start(f32[129,128]{1,0:T(8,128)S(1)} %add.100), channel_id=1, source_target_pairs={{0,4},{1,5},{2,6},{3,7},{4,0},{5,1},{6,2},{7,3},{8,12},{9,13},{10,... | collective-permute-start | bytes 198152 | tf_op jit(solution)/shard_map/ppermute | solution.py:119
  130.2 6.1 %collective-permute-start.19 = (f32[129,128]{1,0:T(8,128)S(1)}, f32[129,128]{1,0:T(8,128)S(1)}, u32[]{:S(2)}, u32[]{:S(2)}) collective-permute-start(f32[129,128]{1,0:T(8,128)S(1)} %add.101), channel_id=1, source_target_pairs={{0,8},{1,9},{2,10},{3,11},{4,12},{5,13},{6,14},{7,15},{8,0},{9,1},... | collective-permute-start | bytes 198152 | tf_op jit(solution)/shard_map/ppermute | solution.py:119

commit v4 on v2

--- a/solution.py
+++ b/solution.py
@@ -59,11 +59,15 @@
     ny = dens_ref.shape[3]
     group = lax.broadcasted_iota(jnp.int32, (nx, ny), 1) // 4
 
-    def body(s, slab):
-        temp = 0.4 * ener_ref[0, s].astype(jnp.float32) / dens_ref[0, s].astype(jnp.float32)
-        return jnp.where(group == s, pltpu.roll(temp, (4 * s + 2) % ny, 1), slab)
-
-    out_ref[0] = lax.fori_loop(0, dens_ref.shape[1], body, jnp.zeros((nx, ny), jnp.float32), unroll=8)
+    def body(s, slabs):
+        shift = (4 * s + 2) % ny
+        dens = pltpu.roll(dens_ref[0, s].astype(jnp.float32), shift, 1)
+        ener = pltpu.roll(ener_ref[0, s].astype(jnp.float32), shift, 1)
+        return jnp.where(group == s, dens, slabs[0]), jnp.where(group == s, ener, slabs[1])
+
+    ones = jnp.ones((nx, ny), jnp.float32)
+    dens, ener = lax.fori_loop(0, dens_ref.shape[1], body, (ones, ones), unroll=8)
+    out_ref[0] = 0.4 * ener / dens
 
 
 def edges_of(state):

time: 172 us -> 172 us (level)
  no operation moved by 1% of the time
where the time goes in v4:
time: 172 us
  other arithmetic  49.9 us (29%)
  starting transfers between devices  41.4 us (24%)
  Pallas kernels  29.5 us (17%)
  waiting for transfers between devices  24.5 us (14%)
  matrix products  17 us (10%)
  local copies, waits for them, and re-layouts  8.68 us (5%)
    ppermute x16, starting transfers between devices, doubling_sum(): lax.ppermute(value, axis, [(i, i ^ step) for i in range(count)])  30.8 us
    pallas_call x1, Pallas kernels, features_of(): pl.pallas_call(feature_kernel, grid=(snaps // block,), in_specs=[pl.Block...  21.6 us
    another operation x4, other arithmetic, tri_solve(): return lax.linalg.triangular_solve(lower, right, left_side=True, lower=True)  21.1 us
    ppermute x16, waiting for transfers between devices, doubling_sum(): lax.ppermute(value, axis, [(i, i ^ step) for i in range(count)])  21 us
    another operation x4, other arithmetic, shards(): low11 = jnp.linalg.cholesky(lead)  12.4 us
    another operation x3, other arithmetic, shards(): low22 = jnp.linalg.cholesky(schur)  12.3 us
    dot_general x1, matrix products, shards(): lax.dot_general(features, features, (((1, 2, 3), (1, 2, 3)), ((), ())), p...  7.98 us
    pallas_call x1, Pallas kernels, edges_of(): pl.pallas_call(edge_kernel, grid=(snaps // block,), in_specs=[pl.BlockSpe...  7.91 us
  transfers between devices with their start and end apart: 20, of which 10 were waited for; matrix products, arithmetic and copies ran while one was open for 15% of the time, Pallas kernels for 0%

profile of v4, /device:TPU:24, one launch (start us, length us, event | category | flops | bytes accessed | tf_op | source)
XLA Modules:
  0.0 172.0 jit_solution(12753299213818289173)
XLA Ops:
  0.6 7.9 %shard_map.30 = f32[8,48,128]{2,1,0:T(8,128)} custom-call(bf16[2,256,48,128]{3,2,1,0:T(8,128)(2,1)} %ener_ref.3, bf16[2,256,48,128]{3,2,1,0:T(8,128)(2,1)} %ener_ref.3), custom_call_target="tpu_custom_call" | custom-call | tf_op jit(solution)/shard_map/pallas_call | solution.py:76
  8.5 2.6 %collective-permute-start.3 = (f32[8,48,128]{2,1,0:T(8,128)}, f32[8,48,128]{2,1,0:T(8,128)S(1)}, u32[]{:S(2)}, u32[]{:S(2)}) collective-permute-start(f32[8,48,128]{2,1,0:T(8,128)} %shard_map.30), channel_id=1, source_target_pairs={{1,0},{2,1},{3,2},{4,3},{5,4},{6,5},{7,6},{8,7},{9,8},{10,9},{11,1... | collective-permute-start | bytes 589832 | tf_op jit(solution)/shard_map/ppermute | solution.py:153
  11.2 5.3 %collective-permute-start.2 = (f32[8,48,128]{2,1,0:T(8,128)}, f32[8,48,128]{2,1,0:T(8,128)S(1)}, u32[]{:S(2)}, u32[]{:S(2)}) collective-permute-start(f32[8,48,128]{2,1,0:T(8,128)} %shard_map.30), channel_id=1, source_target_pairs={{0,1},{1,2},{2,3},{3,4},{4,5},{5,6},{6,7},{7,8},{8,9},{9,10},{10,1... | collective-permute-start | bytes 589832 | tf_op jit(solution)/shard_map/ppermute | solution.py:152
  16.5 2.0 %fusion.19 = (f32[256,2,128]{2,1,0:T(2,128)S(1)}, f32[256,2,128]{2,1,0:T(2,128)S(1)}) fusion(bf16[2,256,48,128]{3,2,1,0:T(8,128)(2,1)} %ener_ref.3), kind=kLoop, calls=%fused_computation.21 | loop fusion | flops 524288 | bytes 1048576 | tf_op jit(solution)/shard_map/div | solution.py:138
  18.5 1.3 collective-permute-start
  19.9 1.3 collective-permute-start.1
  21.2 0.7 fusion.20.yh_ref
  21.9 3.5 %collective-permute-done.1 = f32[256,2,128]{2,1,0:T(2,128)S(1)} collective-permute-done((f32[256,2,128]{2,1,0:T(2,128)S(1)}, f32[256,2,128]{2,1,0:T(2,128)S(1)}, u32[]{:S(2)}, u32[]{:S(2)}) %collective-permute-start.1) | collective-permute-done | bytes 262176 | tf_op jit(solution)/shard_map/ppermute | solution.py:143
  25.4 1.0 pad_maximum_fusion.xh_ref
  26.5 21.6 %shard_map.31 = bf16[256,2,48,128]{3,2,1,0:T(8,128)(2,1)} custom-call(bf16[2,256,48,128]{3,2,1,0:T(8,128)(2,1)} %ener_ref.3, bf16[2,256,48,128]{3,2,1,0:T(8,128)(2,1)} %ener_ref.3, f32[256,4,128]{2,1,0:T(4,128)} %pad_maximum_fusion.xh_ref, f32[8,48,128]{2,1,0:T(8,128)} %fusion.20.yh_ref), custom_call_target="tpu_custom_call" | custom-call | tf_op jit(solution)/shard_map/pallas_call | solution.py:43
  48.1 8.0 %fusion.10 = f32[256,256]{1,0:T(8,128)S(1)} fusion(bf16[256,2,48,128]{3,2,1,0:T(8,128)(2,1)} %shard_map.31), kind=kOutput, calls=%fused_computation.7 | convolution fusion | flops 1610678272 | bytes 6553600 | tf_op jit(solution)/shard_map/dot_general | solution.py:161
  56.1 1.2 gather_fusion
  57.4 4.8 %collective-permute-start.12 = (f32[129,128]{1,0:T(8,128)S(1)}, f32[129,128]{1,0:T(8,128)S(1)}, u32[]{:S(2)}, u32[]{:S(2)}) collective-permute-start(f32[129,128]{1,0:T(8,128)S(1)} %pad_maximum_fusion.4), channel_id=1, source_target_pairs={{0,16},{16,0},{32,48},{48,32},{64,80},{80,64},{96,112},{112,96},{1... | collective-permute-start | bytes 198152 | tf_op jit(solution)/shard_map/ppermute | solution.py:123
  62.3 1.2 collective-permute-done.4
  63.5 2.0 %collective-permute-start.5 = (f32[128,128]{1,0:T(8,128)S(1)}, f32[128,128]{1,0:T(8,128)S(1)}, u32[]{:S(2)}, u32[]{:S(2)}) collective-permute-start(f32[128,128]{1,0:T(8,128)S(1)} %add.86), channel_id=1, source_target_pairs={{0,32},{16,48},{32,0},{48,16},{64,96},{80,112},{96,64},{112,80},{1... | collective-permute-start | bytes 196616 | tf_op jit(solution)/shard_map/ppermute | solution.py:123
  65.7 2.2 %collective-permute-done.5 = f32[128,128]{1,0:T(8,128)S(1)} collective-permute-done((f32[128,128]{1,0:T(8,128)S(1)}, f32[128,128]{1,0:T(8,128)S(1)}, u32[]{:S(2)}, u32[]{:S(2)}) %collective-permute-start.5) | collective-permute-done | bytes 65568 | tf_op jit(solution)/shard_map/ppermute | solution.py:123
  67.9 5.8 %collective-permute-start.6 = (f32[128,128]{1,0:T(8,128)S(1)}, f32[128,128]{1,0:T(8,128)S(1)}, u32[]{:S(2)}, u32[]{:S(2)}) collective-permute-start(f32[128,128]{1,0:T(8,128)S(1)} %add.87), channel_id=1, source_target_pairs={{0,64},{16,80},{32,96},{48,112},{64,0},{80,16},{96,32},{112,48},{1... | collective-permute-start | bytes 196616 | tf_op jit(solution)/shard_map/ppermute | solution.py:123
  73.7 2.2 %collective-permute-start.14 = (f32[129,128]{1,0:T(8,128)S(1)}, f32[129,128]{1,0:T(8,128)S(1)}, u32[]{:S(2)}, u32[]{:S(2)}) collective-permute-start(f32[129,128]{1,0:T(8,128)S(1)} %add.96), channel_id=1, source_target_pairs={{0,64},{16,80},{32,96},{48,112},{64,0},{80,16},{96,32},{112,48},{1... | collective-permute-start | bytes 198152 | tf_op jit(solution)/shard_map/ppermute | solution.py:123
  75.9 0.5 collective-permute-done.6
  76.4 6.2 %collective-permute-start.7 = (f32[128,128]{1,0:T(8,128)S(1)}, f32[128,128]{1,0:T(8,128)S(1)}, u32[]{:S(2)}, u32[]{:S(2)}) collective-permute-start(f32[128,128]{1,0:T(8,128)S(1)} %add.88), channel_id=1, source_target_pairs={{0,128},{16,144},{32,160},{48,176},{64,192},{80,208},{96,224},{112... | collective-permute-start | bytes 196616 | tf_op jit(solution)/shard_map/ppermute | solution.py:123
  82.7 0.8 collective-permute-start.15
  83.5 1.9 %collective-permute-done.7 = f32[128,128]{1,0:T(8,128)S(1)} collective-permute-done((f32[128,128]{1,0:T(8,128)S(1)}, f32[128,128]{1,0:T(8,128)S(1)}, u32[]{:S(2)}, u32[]{:S(2)}) %collective-permute-start.7) | collective-permute-done | bytes 65568 | tf_op jit(solution)/shard_map/ppermute | solution.py:123
  85.5 5.8 %collective-permute-done.15 = f32[129,128]{1,0:T(8,128)S(1)} collective-permute-done((f32[129,128]{1,0:T(8,128)S(1)}, f32[129,128]{1,0:T(8,128)S(1)}, u32[]{:S(2)}, u32[]{:S(2)}) %collective-permute-start.15) | collective-permute-done | bytes 66080 | tf_op jit(solution)/shard_map/ppermute | solution.py:123
  91.5 4.2 %collective-permute-done.16 = f32[129,128]{1,0:T(8,128)S(1)} collective-permute-done((f32[129,128]{1,0:T(8,128)S(1)}, f32[129,128]{1,0:T(8,128)S(1)}, u32[]{:S(2)}, u32[]{:S(2)}) %collective-permute-start.16) | collective-permute-done | bytes 66080 | tf_op jit(solution)/shard_map/ppermute | solution.py:123
  95.7 0.3 collective-permute-start.17
  96.0 1.3 collective-permute-done.9
  97.3 1.6 collective-permute-start.10
  98.9 2.9 %collective-permute-done.17 = f32[129,128]{1,0:T(8,128)S(1)} collective-permute-done((f32[129,128]{1,0:T(8,128)S(1)}, f32[129,128]{1,0:T(8,128)S(1)}, u32[]{:S(2)}, u32[]{:S(2)}) %collective-permute-start.17) | collective-permute-done | bytes 66080 | tf_op jit(solution)/shard_map/ppermute | solution.py:123
  101.8 1.6 collective-permute-start.18
  103.4 1.6 collective-permute-start.11
  105.2 1.0 collective-permute-done.18
  106.2 3.3 %collective-permute-start.19 = (f32[129,128]{1,0:T(8,128)S(1)}, f32[129,128]{1,0:T(8,128)S(1)}, u32[]{:S(2)}, u32[]{:S(2)}) collective-permute-start(f32[129,128]{1,0:T(8,128)S(1)} %add.101), channel_id=1, source_target_pairs={{0,8},{1,9},{2,10},{3,11},{4,12},{5,13},{6,14},{7,15},{8,0},{9,1},... | collective-permute-start | bytes 198152 | tf_op jit(solution)/shard_map/ppermute | solution.py:123
  109.8 11.7 %cholesky.32 = f32[128,128]{1,0:T(8,128)S(1)} custom-call(f32[128,128]{1,0:T(8,128)S(1)} %fusion.34), custom_call_target="Cholesky" | custom-call | tf_op jit(solution)/shard_map/jit(cholesky)/cholesky | solution.py:177
  121.5 0.6 compare_reduce_fusion.1
  122.2 0.7 fusion.25
  122.8 9.8 %custom-call.12 = f32[1,128,128]{1,2,0:T(8,128)S(1)} custom-call(f32[1,128,128]{2,1,0:T(8,128)S(1)} %fusion.25), custom_call_target="InvertDiagBlocksLowerTriangular" | custom-call | tf_op jit(solution)/shard_map/triangular_solve | solution.py:129
  133.1 0.3 fusion.27
  133.6 0.3 slice_subtract_fusion
  134.0 11.6 %cholesky.67 = f32[127,127]{1,0:T(8,128)S(1)} custom-call(f32[127,127]{1,0:T(8,128)S(1)} %fusion.31), custom_call_target="Cholesky" | custom-call | tf_op jit(solution)/shard_map/jit(cholesky)/cholesky | solution.py:181
  145.7 0.6 compare_reduce_fusion
  146.3 0.7 fusion.26
  147.0 10.0 %custom-call.13 = f32[1,127,127]{1,2,0:T(8,128)S(1)} custom-call(f32[1,127,127]{2,1,0:T(8,128)S(1)} %fusion.26), custom_call_target="InvertDiagBlocksLowerTriangular" | custom-call | tf_op jit(solution)/shard_map/triangular_solve | solution.py:129
  157.0 0.3 fusion.29
  157.3 0.3 convolution_negate_fusion
  157.7 0.4 fusion.14
  158.2 1.1 fusion.23
  159.3 5.9 %fusion.4 = bf16[255,2,48,128]{3,0,2,1:T(8,128)(2,1)S(1)} fusion(bf16[256,2,48,128]{3,2,1,0:T(8,128)(2,1)} %shard_map.31, bf16[255,255]{1,0:T(8,128)(2,1)S(1)} %fusion.24), kind=kOutput, calls=%fused_computation.5 | convolution fusion | flops 1607454720 | bytes 12688386 | tf_op jit(solution)/shard_map/dot_general | solution.py:196
  165.2 6.7 %copy.28 = bf16[255,2,48,128]{3,2,1,0:T(8,128)(2,1)} copy(bf16[255,2,48,128]{3,0,2,1:T(8,128)(2,1)S(1)} %fusion.4) | data formatting | bytes 12533760
  (55 shorter events, 2.2 us)
Async XLA Ops:
  8.5 12.7 %collective-permute-start.3 = (f32[8,48,128]{2,1,0:T(8,128)}, f32[8,48,128]{2,1,0:T(8,128)S(1)}, u32[]{:S(2)}, u32[]{:S(2)}) collective-permute-start(f32[8,48,128]{2,1,0:T(8,128)} %shard_map.30), channel_id=1, source_target_pairs={{1,0},{2,1},{3,2},{4,3},{5,4},{6,5},{7,6},{8,7},{9,8},{10,9},{11,1... | collective-permute-start | bytes 589832 | tf_op jit(solution)/shard_map/ppermute | solution.py:153
  11.2 10.0 %collective-permute-start.2 = (f32[8,48,128]{2,1,0:T(8,128)}, f32[8,48,128]{2,1,0:T(8,128)S(1)}, u32[]{:S(2)}, u32[]{:S(2)}) collective-permute-start(f32[8,48,128]{2,1,0:T(8,128)} %shard_map.30), channel_id=1, source_target_pairs={{0,1},{1,2},{2,3},{3,4},{4,5},{5,6},{6,7},{7,8},{8,9},{9,10},{10,1... | collective-permute-start | bytes 589832 | tf_op jit(solution)/shard_map/ppermute | solution.py:152
  18.5 3.4 %collective-permute-start = (f32[256,2,128]{2,1,0:T(2,128)S(1)}, f32[256,2,128]{2,1,0:T(2,128)S(1)}, u32[]{:S(2)}, u32[]{:S(2)}) collective-permute-start(f32[256,2,128]{2,1,0:T(2,128)S(1)} %get-tuple-element.6), channel_id=1, source_target_pairs={{0,16},{16,32},{32,48},{48,64},{64,80},{80,96},{96,112},{112,128},... | collective-permute-start | bytes 786440 | tf_op jit(solution)/shard_map/ppermute | solution.py:142
  19.9 5.6 %collective-permute-start.1 = (f32[256,2,128]{2,1,0:T(2,128)S(1)}, f32[256,2,128]{2,1,0:T(2,128)S(1)}, u32[]{:S(2)}, u32[]{:S(2)}) collective-permute-start(f32[256,2,128]{2,1,0:T(2,128)S(1)} %get-tuple-element.7), channel_id=1, source_target_pairs={{16,0},{32,16},{48,32},{64,48},{80,64},{96,80},{112,96},{128,112},... | collective-permute-start | bytes 786440 | tf_op jit(solution)/shard_map/ppermute | solution.py:143
  57.4 8.1 %collective-permute-start.12 = (f32[129,128]{1,0:T(8,128)S(1)}, f32[129,128]{1,0:T(8,128)S(1)}, u32[]{:S(2)}, u32[]{:S(2)}) collective-permute-start(f32[129,128]{1,0:T(8,128)S(1)} %pad_maximum_fusion.4), channel_id=1, source_target_pairs={{0,16},{16,0},{32,48},{48,32},{64,80},{80,64},{96,112},{112,96},{1... | collective-permute-start | bytes 198152 | tf_op jit(solution)/shard_map/ppermute | solution.py:123
  62.2 1.3 collective-permute-start.4
  63.5 4.4 %collective-permute-start.5 = (f32[128,128]{1,0:T(8,128)S(1)}, f32[128,128]{1,0:T(8,128)S(1)}, u32[]{:S(2)}, u32[]{:S(2)}) collective-permute-start(f32[128,128]{1,0:T(8,128)S(1)} %add.86), channel_id=1, source_target_pairs={{0,32},{16,48},{32,0},{48,16},{64,96},{80,112},{96,64},{112,80},{1... | collective-permute-start | bytes 196616 | tf_op jit(solution)/shard_map/ppermute | solution.py:123
  65.5 8.2 %collective-permute-start.13 = (f32[129,128]{1,0:T(8,128)S(1)}, f32[129,128]{1,0:T(8,128)S(1)}, u32[]{:S(2)}, u32[]{:S(2)}) collective-permute-start(f32[129,128]{1,0:T(8,128)S(1)} %fusion.42), channel_id=1, source_target_pairs={{0,32},{16,48},{32,0},{48,16},{64,96},{80,112},{96,64},{112,80},{1... | collective-permute-start | bytes 198152 | tf_op jit(solution)/shard_map/ppermute | solution.py:123
  67.9 8.5 %collective-permute-start.6 = (f32[128,128]{1,0:T(8,128)S(1)}, f32[128,128]{1,0:T(8,128)S(1)}, u32[]{:S(2)}, u32[]{:S(2)}) collective-permute-start(f32[128,128]{1,0:T(8,128)S(1)} %add.87), channel_id=1, source_target_pairs={{0,64},{16,80},{32,96},{48,112},{64,0},{80,16},{96,32},{112,48},{1... | collective-permute-start | bytes 196616 | tf_op jit(solution)/shard_map/ppermute | solution.py:123
  73.7 8.9 %collective-permute-start.14 = (f32[129,128]{1,0:T(8,128)S(1)}, f32[129,128]{1,0:T(8,128)S(1)}, u32[]{:S(2)}, u32[]{:S(2)}) collective-permute-start(f32[129,128]{1,0:T(8,128)S(1)} %add.96), channel_id=1, source_target_pairs={{0,64},{16,80},{32,96},{48,112},{64,0},{80,16},{96,32},{112,48},{1... | collective-permute-start | bytes 198152 | tf_op jit(solution)/shard_map/ppermute | solution.py:123
  76.4 8.9 %collective-permute-start.7 = (f32[128,128]{1,0:T(8,128)S(1)}, f32[128,128]{1,0:T(8,128)S(1)}, u32[]{:S(2)}, u32[]{:S(2)}) collective-permute-start(f32[128,128]{1,0:T(8,128)S(1)} %add.88), channel_id=1, source_target_pairs={{0,128},{16,144},{32,160},{48,176},{64,192},{80,208},{96,224},{112... | collective-permute-start | bytes 196616 | tf_op jit(solution)/shard_map/ppermute | solution.py:123
  82.7 8.6 %collective-permute-start.15 = (f32[129,128]{1,0:T(8,128)S(1)}, f32[129,128]{1,0:T(8,128)S(1)}, u32[]{:S(2)}, u32[]{:S(2)}) collective-permute-start(f32[129,128]{1,0:T(8,128)S(1)} %add.97), channel_id=1, source_target_pairs={{0,128},{16,144},{32,160},{48,176},{64,192},{80,208},{96,224},{112... | collective-permute-start | bytes 198152 | tf_op jit(solution)/shard_map/ppermute | solution.py:123
  85.4 6.0 %collective-permute-start.8 = (f32[128,128]{1,0:T(8,128)S(1)}, f32[128,128]{1,0:T(8,128)S(1)}, u32[]{:S(2)}, u32[]{:S(2)}) collective-permute-start(f32[128,128]{1,0:T(8,128)S(1)} %add.89), channel_id=1, source_target_pairs={{0,1},{1,0},{2,3},{3,2},{4,5},{5,4},{6,7},{7,6},{8,9},{9,8},{10,11... | collective-permute-start | bytes 196616 | tf_op jit(solution)/shard_map/ppermute | solution.py:123
  91.3 4.4 %collective-permute-start.16 = (f32[129,128]{1,0:T(8,128)S(1)}, f32[129,128]{1,0:T(8,128)S(1)}, u32[]{:S(2)}, u32[]{:S(2)}) collective-permute-start(f32[129,128]{1,0:T(8,128)S(1)} %add.98), channel_id=1, source_target_pairs={{0,1},{1,0},{2,3},{3,2},{4,5},{5,4},{6,7},{7,6},{8,9},{9,8},{10,11... | collective-permute-start | bytes 198152 | tf_op jit(solution)/shard_map/ppermute | solution.py:123
  91.4 5.9 %collective-permute-start.9 = (f32[128,128]{1,0:T(8,128)S(1)}, f32[128,128]{1,0:T(8,128)S(1)}, u32[]{:S(2)}, u32[]{:S(2)}) collective-permute-start(f32[128,128]{1,0:T(8,128)S(1)} %add.90), channel_id=1, source_target_pairs={{0,2},{1,3},{2,0},{3,1},{4,6},{5,7},{6,4},{7,5},{8,10},{9,11},{10,... | collective-permute-start | bytes 196616 | tf_op jit(solution)/shard_map/ppermute | solution.py:123
  95.7 6.1 %collective-permute-start.17 = (f32[129,128]{1,0:T(8,128)S(1)}, f32[129,128]{1,0:T(8,128)S(1)}, u32[]{:S(2)}, u32[]{:S(2)}) collective-permute-start(f32[129,128]{1,0:T(8,128)S(1)} %add.99), channel_id=1, source_target_pairs={{0,2},{1,3},{2,0},{3,1},{4,6},{5,7},{6,4},{7,5},{8,10},{9,11},{10,... | collective-permute-start | bytes 198152 | tf_op jit(solution)/shard_map/ppermute | solution.py:123
  97.3 6.1 %collective-permute-start.10 = (f32[128,128]{1,0:T(8,128)S(1)}, f32[128,128]{1,0:T(8,128)S(1)}, u32[]{:S(2)}, u32[]{:S(2)}) collective-permute-start(f32[128,128]{1,0:T(8,128)S(1)} %add.91), channel_id=1, source_target_pairs={{0,4},{1,5},{2,6},{3,7},{4,0},{5,1},{6,2},{7,3},{8,12},{9,13},{10,... | collective-permute-start | bytes 196616 | tf_op jit(solution)/shard_map/ppermute | solution.py:123
  101.8 4.4 %collective-permute-start.18 = (f32[129,128]{1,0:T(8,128)S(1)}, f32[129,128]{1,0:T(8,128)S(1)}, u32[]{:S(2)}, u32[]{:S(2)}) collective-permute-start(f32[129,128]{1,0:T(8,128)S(1)} %add.100), channel_id=1, source_target_pairs={{0,4},{1,5},{2,6},{3,7},{4,0},{5,1},{6,2},{7,3},{8,12},{9,13},{10,... | collective-permute-start | bytes 198152 | tf_op jit(solution)/shard_map/ppermute | solution.py:123
  103.4 6.1 %collective-permute-start.11 = (f32[128,128]{1,0:T(8,128)S(1)}, f32[128,128]{1,0:T(8,128)S(1)}, u32[]{:S(2)}, u32[]{:S(2)}) collective-permute-start(f32[128,128]{1,0:T(8,128)S(1)} %add.92), channel_id=1, source_target_pairs={{0,8},{1,9},{2,10},{3,11},{4,12},{5,13},{6,14},{7,15},{8,0},{9,1},... | collective-permute-start | bytes 196616 | tf_op jit(solution)/shard_map/ppermute | solution.py:123
  106.2 26.8 %collective-permute-start.19 = (f32[129,128]{1,0:T(8,128)S(1)}, f32[129,128]{1,0:T(8,128)S(1)}, u32[]{:S(2)}, u32[]{:S(2)}) collective-permute-start(f32[129,128]{1,0:T(8,128)S(1)} %add.101), channel_id=1, source_target_pairs={{0,8},{1,9},{2,10},{3,11},{4,12},{5,13},{6,14},{7,15},{8,0},{9,1},... | collective-permute-start | bytes 198152 | tf_op jit(solution)/shard_map/ppermute | solution.py:123

commit v5 on v2

--- a/solution.py
+++ b/solution.py
@@ -13,7 +13,18 @@
     ny = dens_ref.shape[3]
     lanes = yh_ref.shape[2]
     rows = lax.broadcasted_iota(jnp.int32, (nx, ny), 0)
-    cols = lax.broadcasted_iota(jnp.int32, (nx, ny), 1)
+    src = lax.broadcasted_iota(jnp.int32, (ny, ny), 0)
+    dst = lax.broadcasted_iota(jnp.int32, (ny, ny), 1)
+    gap = src - dst
+    inner = jnp.where(gap == -2, 1.0, 0.0) - jnp.where(gap == -1, 8.0, 0.0)
+    inner = inner + jnp.where(gap == 1, 8.0, 0.0) - jnp.where(gap == 2, 1.0, 0.0)
+
+    def tap(i, j, value):
+        return jnp.where((src == i) & (dst == j), value, 0.0)
+
+    outer = tap(ny - 2, 0, 1.0) + tap(ny - 1, 0, -8.0) + tap(ny - 1, 1, 1.0)
+    outer = outer + tap(0, ny - 2, -1.0) + tap(0, ny - 1, 8.0) + tap(1, ny - 1, -1.0)
+    stencil = jnp.concatenate([inner, outer], axis=0)
 
     def body(s, carry):
         temp = 0.4 * ener_ref[0, s].astype(jnp.float32) / dens_ref[0, s].astype(jnp.float32)
@@ -23,12 +34,13 @@
         up1 = jnp.where(rows == 0, xh[1:2], pltpu.roll(temp, 1, 0))
         dn1 = jnp.where(rows == nx - 1, xh[2:3], pltpu.roll(temp, nx - 1, 0))
         dn2 = jnp.where(rows == nx - 2, xh[2:3], jnp.where(rows == nx - 1, xh[3:4], pltpu.roll(temp, nx - 2, 0)))
-        lf2 = pltpu.roll(jnp.where(cols >= ny - 2, halo, temp), 2, 1)
-        lf1 = pltpu.roll(jnp.where(cols == ny - 1, halo, temp), 1, 1)
-        rt1 = pltpu.roll(jnp.where(cols == 0, halo, temp), ny - 1, 1)
-        rt2 = pltpu.roll(jnp.where(cols < 2, halo, temp), ny - 2, 1)
         grad_x = (up2 - 8.0 * up1 + 8.0 * dn1 - dn2) / 12.0
-        grad_y = (lf2 - 8.0 * lf1 + 8.0 * rt1 - rt2) / 12.0
+        grad_y = jnp.dot(
+            jnp.concatenate([temp, halo], axis=1),
+            stencil,
+            precision=lax.Precision.HIGHEST,
+            preferred_element_type=jnp.float32,
+        ) / 12.0
         out_ref[s, 0] = grad_x.astype(out_ref.dtype)
         out_ref[s, 1] = grad_y.astype(out_ref.dtype)
         return carry

time: 172 us -> 174 us (1.012)
  no operation moved by 1% of the time
where the time goes in v5:
time: 174 us; the launch traced here: 173 us
  other arithmetic  49.9 us (29%)
  starting transfers between devices  41.5 us (24%)
  Pallas kernels  30.7 us (18%)
  waiting for transfers between devices  24.2 us (14%)
  matrix products  17 us (10%)
  local copies, waits for them, and re-layouts  8.68 us (5%)
    ppermute x16, starting transfers between devices, doubling_sum(): lax.ppermute(value, axis, [(i, i ^ step) for i in range(count)])  30.9 us
    pallas_call x1, Pallas kernels, features_of(): pl.pallas_call(feature_kernel, grid=(snaps // block,), in_specs=[pl.Block...  22.8 us
    another operation x4, other arithmetic, tri_solve(): return lax.linalg.triangular_solve(lower, right, left_side=True, lower=True)  21.1 us
    ppermute x16, waiting for transfers between devices, doubling_sum(): lax.ppermute(value, axis, [(i, i ^ step) for i in range(count)])  20.7 us
    another operation x4, other arithmetic, shards(): low11 = jnp.linalg.cholesky(lead)  12.4 us
    another operation x3, other arithmetic, shards(): low22 = jnp.linalg.cholesky(schur)  12.3 us
    dot_general x1, matrix products, shards(): lax.dot_general(features, features, (((1, 2, 3), (1, 2, 3)), ((), ())), p...  7.98 us
    pallas_call x1, Pallas kernels, edges_of(): pl.pallas_call(edge_kernel, grid=(snaps // block,), in_specs=[pl.BlockSpe...  7.92 us
  transfers between devices with their start and end apart: 20, of which 10 were waited for; matrix products, arithmetic and copies ran while one was open for 15% of the time, Pallas kernels for 0%

profile of v5, /device:TPU:24, one launch (start us, length us, event | category | flops | bytes accessed | tf_op | source)
XLA Modules:
  0.0 172.9 jit_solution(7072891792785710409)
XLA Ops:
  0.6 7.9 %shard_map.30 = f32[8,48,128]{2,1,0:T(8,128)} custom-call(bf16[2,256,48,128]{3,2,1,0:T(8,128)(2,1)} %ener_ref.3, bf16[2,256,48,128]{3,2,1,0:T(8,128)(2,1)} %ener_ref.3), custom_call_target="tpu_custom_call" | custom-call | tf_op jit(solution)/shard_map/pallas_call | solution.py:84
  8.6 2.6 %collective-permute-start.3 = (f32[8,48,128]{2,1,0:T(8,128)}, f32[8,48,128]{2,1,0:T(8,128)S(1)}, u32[]{:S(2)}, u32[]{:S(2)}) collective-permute-start(f32[8,48,128]{2,1,0:T(8,128)} %shard_map.30), channel_id=1, source_target_pairs={{1,0},{2,1},{3,2},{4,3},{5,4},{6,5},{7,6},{8,7},{9,8},{10,9},{11,1... | collective-permute-start | bytes 589832 | tf_op jit(solution)/shard_map/ppermute | solution.py:161
  11.2 5.3 %collective-permute-start.2 = (f32[8,48,128]{2,1,0:T(8,128)}, f32[8,48,128]{2,1,0:T(8,128)S(1)}, u32[]{:S(2)}, u32[]{:S(2)}) collective-permute-start(f32[8,48,128]{2,1,0:T(8,128)} %shard_map.30), channel_id=1, source_target_pairs={{0,1},{1,2},{2,3},{3,4},{4,5},{5,6},{6,7},{7,8},{8,9},{9,10},{10,1... | collective-permute-start | bytes 589832 | tf_op jit(solution)/shard_map/ppermute | solution.py:160
  16.5 2.0 %fusion.19 = (f32[256,2,128]{2,1,0:T(2,128)S(1)}, f32[256,2,128]{2,1,0:T(2,128)S(1)}) fusion(bf16[2,256,48,128]{3,2,1,0:T(8,128)(2,1)} %ener_ref.3), kind=kLoop, calls=%fused_computation.21 | loop fusion | flops 524288 | bytes 1048576 | tf_op jit(solution)/shard_map/div | solution.py:146
  18.6 1.3 collective-permute-start
  19.9 1.3 collective-permute-start.1
  21.2 0.7 fusion.20.yh_ref
  21.9 3.5 %collective-permute-done.1 = f32[256,2,128]{2,1,0:T(2,128)S(1)} collective-permute-done((f32[256,2,128]{2,1,0:T(2,128)S(1)}, f32[256,2,128]{2,1,0:T(2,128)S(1)}, u32[]{:S(2)}, u32[]{:S(2)}) %collective-permute-start.1) | collective-permute-done | bytes 262176 | tf_op jit(solution)/shard_map/ppermute | solution.py:151
  25.4 1.0 pad_maximum_fusion.xh_ref
  26.5 22.8 %shard_map.31 = bf16[256,2,48,128]{3,2,1,0:T(8,128)(2,1)} custom-call(bf16[2,256,48,128]{3,2,1,0:T(8,128)(2,1)} %ener_ref.3, bf16[2,256,48,128]{3,2,1,0:T(8,128)(2,1)} %ener_ref.3, f32[256,4,128]{2,1,0:T(4,128)} %pad_maximum_fusion.xh_ref, f32[8,48,128]{2,1,0:T(8,128)} %fusion.20.yh_ref), custom_call_target="tpu_custom_call" | custom-call | tf_op jit(solution)/shard_map/pallas_call | solution.py:55
  49.2 8.0 %fusion.10 = f32[256,256]{1,0:T(8,128)S(1)} fusion(bf16[256,2,48,128]{3,2,1,0:T(8,128)(2,1)} %shard_map.31), kind=kOutput, calls=%fused_computation.7 | convolution fusion | flops 1610678272 | bytes 6553600 | tf_op jit(solution)/shard_map/dot_general | solution.py:169
  57.2 1.2 gather_fusion
  58.5 4.8 %collective-permute-start.12 = (f32[129,128]{1,0:T(8,128)S(1)}, f32[129,128]{1,0:T(8,128)S(1)}, u32[]{:S(2)}, u32[]{:S(2)}) collective-permute-start(f32[129,128]{1,0:T(8,128)S(1)} %pad_maximum_fusion.4), channel_id=1, source_target_pairs={{0,16},{16,0},{32,48},{48,32},{64,80},{80,64},{96,112},{112,96},{1... | collective-permute-start | bytes 198152 | tf_op jit(solution)/shard_map/ppermute | solution.py:131
  63.4 1.2 collective-permute-done.4
  64.6 2.0 %collective-permute-start.5 = (f32[128,128]{1,0:T(8,128)S(1)}, f32[128,128]{1,0:T(8,128)S(1)}, u32[]{:S(2)}, u32[]{:S(2)}) collective-permute-start(f32[128,128]{1,0:T(8,128)S(1)} %add.86), channel_id=1, source_target_pairs={{0,32},{16,48},{32,0},{48,16},{64,96},{80,112},{96,64},{112,80},{1... | collective-permute-start | bytes 196616 | tf_op jit(solution)/shard_map/ppermute | solution.py:131
  66.8 2.2 %collective-permute-done.5 = f32[128,128]{1,0:T(8,128)S(1)} collective-permute-done((f32[128,128]{1,0:T(8,128)S(1)}, f32[128,128]{1,0:T(8,128)S(1)}, u32[]{:S(2)}, u32[]{:S(2)}) %collective-permute-start.5) | collective-permute-done | bytes 65568 | tf_op jit(solution)/shard_map/ppermute | solution.py:131
  69.1 5.8 %collective-permute-start.6 = (f32[128,128]{1,0:T(8,128)S(1)}, f32[128,128]{1,0:T(8,128)S(1)}, u32[]{:S(2)}, u32[]{:S(2)}) collective-permute-start(f32[128,128]{1,0:T(8,128)S(1)} %add.87), channel_id=1, source_target_pairs={{0,64},{16,80},{32,96},{48,112},{64,0},{80,16},{96,32},{112,48},{1... | collective-permute-start | bytes 196616 | tf_op jit(solution)/shard_map/ppermute | solution.py:131
  74.9 2.2 %collective-permute-start.14 = (f32[129,128]{1,0:T(8,128)S(1)}, f32[129,128]{1,0:T(8,128)S(1)}, u32[]{:S(2)}, u32[]{:S(2)}) collective-permute-start(f32[129,128]{1,0:T(8,128)S(1)} %add.96), channel_id=1, source_target_pairs={{0,64},{16,80},{32,96},{48,112},{64,0},{80,16},{96,32},{112,48},{1... | collective-permute-start | bytes 198152 | tf_op jit(solution)/shard_map/ppermute | solution.py:131
  77.1 0.5 collective-permute-done.6
  77.6 6.2 %collective-permute-start.7 = (f32[128,128]{1,0:T(8,128)S(1)}, f32[128,128]{1,0:T(8,128)S(1)}, u32[]{:S(2)}, u32[]{:S(2)}) collective-permute-start(f32[128,128]{1,0:T(8,128)S(1)} %add.88), channel_id=1, source_target_pairs={{0,128},{16,144},{32,160},{48,176},{64,192},{80,208},{96,224},{112... | collective-permute-start | bytes 196616 | tf_op jit(solution)/shard_map/ppermute | solution.py:131
  83.8 0.8 collective-permute-start.15
  84.6 1.9 %collective-permute-done.7 = f32[128,128]{1,0:T(8,128)S(1)} collective-permute-done((f32[128,128]{1,0:T(8,128)S(1)}, f32[128,128]{1,0:T(8,128)S(1)}, u32[]{:S(2)}, u32[]{:S(2)}) %collective-permute-start.7) | collective-permute-done | bytes 65568 | tf_op jit(solution)/shard_map/ppermute | solution.py:131
  86.6 5.8 %collective-permute-done.15 = f32[129,128]{1,0:T(8,128)S(1)} collective-permute-done((f32[129,128]{1,0:T(8,128)S(1)}, f32[129,128]{1,0:T(8,128)S(1)}, u32[]{:S(2)}, u32[]{:S(2)}) %collective-permute-start.15) | collective-permute-done | bytes 66080 | tf_op jit(solution)/shard_map/ppermute | solution.py:131
  92.6 0.3 collective-permute-start.9
  92.8 4.0 %collective-permute-done.16 = f32[129,128]{1,0:T(8,128)S(1)} collective-permute-done((f32[129,128]{1,0:T(8,128)S(1)}, f32[129,128]{1,0:T(8,128)S(1)}, u32[]{:S(2)}, u32[]{:S(2)}) %collective-permute-start.16) | collective-permute-done | bytes 66080 | tf_op jit(solution)/shard_map/ppermute | solution.py:131
  96.9 1.7 collective-permute-done.9
  98.6 1.6 collective-permute-start.10
  100.2 2.5 %collective-permute-done.17 = f32[129,128]{1,0:T(8,128)S(1)} collective-permute-done((f32[129,128]{1,0:T(8,128)S(1)}, f32[129,128]{1,0:T(8,128)S(1)}, u32[]{:S(2)}, u32[]{:S(2)}) %collective-permute-start.17) | collective-permute-done | bytes 66080 | tf_op jit(solution)/shard_map/ppermute | solution.py:131
  102.8 1.6 collective-permute-start.18
  104.4 1.7 %collective-permute-start.11 = (f32[128,128]{1,0:T(8,128)S(1)}, f32[128,128]{1,0:T(8,128)S(1)}, u32[]{:S(2)}, u32[]{:S(2)}) collective-permute-start(f32[128,128]{1,0:T(8,128)S(1)} %add.92), channel_id=1, source_target_pairs={{0,8},{1,9},{2,10},{3,11},{4,12},{5,13},{6,14},{7,15},{8,0},{9,1},... | collective-permute-start | bytes 196616 | tf_op jit(solution)/shard_map/ppermute | solution.py:131
  106.2 0.9 collective-permute-done.18
  107.2 3.3 %collective-permute-start.19 = (f32[129,128]{1,0:T(8,128)S(1)}, f32[129,128]{1,0:T(8,128)S(1)}, u32[]{:S(2)}, u32[]{:S(2)}) collective-permute-start(f32[129,128]{1,0:T(8,128)S(1)} %add.101), channel_id=1, source_target_pairs={{0,8},{1,9},{2,10},{3,11},{4,12},{5,13},{6,14},{7,15},{8,0},{9,1},... | collective-permute-start | bytes 198152 | tf_op jit(solution)/shard_map/ppermute | solution.py:131
  110.8 11.7 %cholesky.32 = f32[128,128]{1,0:T(8,128)S(1)} custom-call(f32[128,128]{1,0:T(8,128)S(1)} %fusion.34), custom_call_target="Cholesky" | custom-call | tf_op jit(solution)/shard_map/jit(cholesky)/cholesky | solution.py:185
  122.5 0.6 compare_reduce_fusion.1
  123.1 0.7 fusion.25
  123.8 9.8 %custom-call.12 = f32[1,128,128]{1,2,0:T(8,128)S(1)} custom-call(f32[1,128,128]{2,1,0:T(8,128)S(1)} %fusion.25), custom_call_target="InvertDiagBlocksLowerTriangular" | custom-call | tf_op jit(solution)/shard_map/triangular_solve | solution.py:137
  134.0 0.3 fusion.27
  134.6 0.3 slice_subtract_fusion
  135.0 11.6 %cholesky.67 = f32[127,127]{1,0:T(8,128)S(1)} custom-call(f32[127,127]{1,0:T(8,128)S(1)} %fusion.31), custom_call_target="Cholesky" | custom-call | tf_op jit(solution)/shard_map/jit(cholesky)/cholesky | solution.py:189
  146.7 0.6 compare_reduce_fusion
  147.3 0.7 fusion.26
  148.0 10.0 %custom-call.13 = f32[1,127,127]{1,2,0:T(8,128)S(1)} custom-call(f32[1,127,127]{2,1,0:T(8,128)S(1)} %fusion.26), custom_call_target="InvertDiagBlocksLowerTriangular" | custom-call | tf_op jit(solution)/shard_map/triangular_solve | solution.py:137
  157.9 0.3 fusion.29
  158.3 0.3 convolution_negate_fusion
  158.7 0.4 fusion.14
  159.1 1.1 fusion.23
  160.3 5.9 %fusion.4 = bf16[255,2,48,128]{3,0,2,1:T(8,128)(2,1)S(1)} fusion(bf16[256,2,48,128]{3,2,1,0:T(8,128)(2,1)} %shard_map.31, bf16[255,255]{1,0:T(8,128)(2,1)S(1)} %fusion.24), kind=kOutput, calls=%fused_computation.5 | convolution fusion | flops 1607454720 | bytes 12688386 | tf_op jit(solution)/shard_map/dot_general | solution.py:204
  166.2 6.7 %copy.28 = bf16[255,2,48,128]{3,2,1,0:T(8,128)(2,1)} copy(bf16[255,2,48,128]{3,0,2,1:T(8,128)(2,1)S(1)} %fusion.4) | data formatting | bytes 12533760
  (55 shorter events, 2.2 us)
Async XLA Ops:
  8.6 12.7 %collective-permute-start.3 = (f32[8,48,128]{2,1,0:T(8,128)}, f32[8,48,128]{2,1,0:T(8,128)S(1)}, u32[]{:S(2)}, u32[]{:S(2)}) collective-permute-start(f32[8,48,128]{2,1,0:T(8,128)} %shard_map.30), channel_id=1, source_target_pairs={{1,0},{2,1},{3,2},{4,3},{5,4},{6,5},{7,6},{8,7},{9,8},{10,9},{11,1... | collective-permute-start | bytes 589832 | tf_op jit(solution)/shard_map/ppermute | solution.py:161
  11.2 10.0 %collective-permute-start.2 = (f32[8,48,128]{2,1,0:T(8,128)}, f32[8,48,128]{2,1,0:T(8,128)S(1)}, u32[]{:S(2)}, u32[]{:S(2)}) collective-permute-start(f32[8,48,128]{2,1,0:T(8,128)} %shard_map.30), channel_id=1, source_target_pairs={{0,1},{1,2},{2,3},{3,4},{4,5},{5,6},{6,7},{7,8},{8,9},{9,10},{10,1... | collective-permute-start | bytes 589832 | tf_op jit(solution)/shard_map/ppermute | solution.py:160
  18.6 3.4 %collective-permute-start = (f32[256,2,128]{2,1,0:T(2,128)S(1)}, f32[256,2,128]{2,1,0:T(2,128)S(1)}, u32[]{:S(2)}, u32[]{:S(2)}) collective-permute-start(f32[256,2,128]{2,1,0:T(2,128)S(1)} %get-tuple-element.6), channel_id=1, source_target_pairs={{0,16},{16,32},{32,48},{48,64},{64,80},{80,96},{96,112},{112,128},... | collective-permute-start | bytes 786440 | tf_op jit(solution)/shard_map/ppermute | solution.py:150
  19.9 5.6 %collective-permute-start.1 = (f32[256,2,128]{2,1,0:T(2,128)S(1)}, f32[256,2,128]{2,1,0:T(2,128)S(1)}, u32[]{:S(2)}, u32[]{:S(2)}) collective-permute-start(f32[256,2,128]{2,1,0:T(2,128)S(1)} %get-tuple-element.7), channel_id=1, source_target_pairs={{16,0},{32,16},{48,32},{64,48},{80,64},{96,80},{112,96},{128,112},... | collective-permute-start | bytes 786440 | tf_op jit(solution)/shard_map/ppermute | solution.py:151
  58.5 8.1 %collective-permute-start.12 = (f32[129,128]{1,0:T(8,128)S(1)}, f32[129,128]{1,0:T(8,128)S(1)}, u32[]{:S(2)}, u32[]{:S(2)}) collective-permute-start(f32[129,128]{1,0:T(8,128)S(1)} %pad_maximum_fusion.4), channel_id=1, source_target_pairs={{0,16},{16,0},{32,48},{48,32},{64,80},{80,64},{96,112},{112,96},{1... | collective-permute-start | bytes 198152 | tf_op jit(solution)/shard_map/ppermute | solution.py:131
  63.3 1.3 collective-permute-start.4
  64.6 4.5 %collective-permute-start.5 = (f32[128,128]{1,0:T(8,128)S(1)}, f32[128,128]{1,0:T(8,128)S(1)}, u32[]{:S(2)}, u32[]{:S(2)}) collective-permute-start(f32[128,128]{1,0:T(8,128)S(1)} %add.86), channel_id=1, source_target_pairs={{0,32},{16,48},{32,0},{48,16},{64,96},{80,112},{96,64},{112,80},{1... | collective-permute-start | bytes 196616 | tf_op jit(solution)/shard_map/ppermute | solution.py:131
  66.6 8.2 %collective-permute-start.13 = (f32[129,128]{1,0:T(8,128)S(1)}, f32[129,128]{1,0:T(8,128)S(1)}, u32[]{:S(2)}, u32[]{:S(2)}) collective-permute-start(f32[129,128]{1,0:T(8,128)S(1)} %fusion.42), channel_id=1, source_target_pairs={{0,32},{16,48},{32,0},{48,16},{64,96},{80,112},{96,64},{112,80},{1... | collective-permute-start | bytes 198152 | tf_op jit(solution)/shard_map/ppermute | solution.py:131
  69.1 8.5 %collective-permute-start.6 = (f32[128,128]{1,0:T(8,128)S(1)}, f32[128,128]{1,0:T(8,128)S(1)}, u32[]{:S(2)}, u32[]{:S(2)}) collective-permute-start(f32[128,128]{1,0:T(8,128)S(1)} %add.87), channel_id=1, source_target_pairs={{0,64},{16,80},{32,96},{48,112},{64,0},{80,16},{96,32},{112,48},{1... | collective-permute-start | bytes 196616 | tf_op jit(solution)/shard_map/ppermute | solution.py:131
  74.9 8.9 %collective-permute-start.14 = (f32[129,128]{1,0:T(8,128)S(1)}, f32[129,128]{1,0:T(8,128)S(1)}, u32[]{:S(2)}, u32[]{:S(2)}) collective-permute-start(f32[129,128]{1,0:T(8,128)S(1)} %add.96), channel_id=1, source_target_pairs={{0,64},{16,80},{32,96},{48,112},{64,0},{80,16},{96,32},{112,48},{1... | collective-permute-start | bytes 198152 | tf_op jit(solution)/shard_map/ppermute | solution.py:131
  77.6 8.9 %collective-permute-start.7 = (f32[128,128]{1,0:T(8,128)S(1)}, f32[128,128]{1,0:T(8,128)S(1)}, u32[]{:S(2)}, u32[]{:S(2)}) collective-permute-start(f32[128,128]{1,0:T(8,128)S(1)} %add.88), channel_id=1, source_target_pairs={{0,128},{16,144},{32,160},{48,176},{64,192},{80,208},{96,224},{112... | collective-permute-start | bytes 196616 | tf_op jit(solution)/shard_map/ppermute | solution.py:131
  83.8 8.6 %collective-permute-start.15 = (f32[129,128]{1,0:T(8,128)S(1)}, f32[129,128]{1,0:T(8,128)S(1)}, u32[]{:S(2)}, u32[]{:S(2)}) collective-permute-start(f32[129,128]{1,0:T(8,128)S(1)} %add.97), channel_id=1, source_target_pairs={{0,128},{16,144},{32,160},{48,176},{64,192},{80,208},{96,224},{112... | collective-permute-start | bytes 198152 | tf_op jit(solution)/shard_map/ppermute | solution.py:131
  86.5 6.0 %collective-permute-start.8 = (f32[128,128]{1,0:T(8,128)S(1)}, f32[128,128]{1,0:T(8,128)S(1)}, u32[]{:S(2)}, u32[]{:S(2)}) collective-permute-start(f32[128,128]{1,0:T(8,128)S(1)} %add.89), channel_id=1, source_target_pairs={{0,1},{1,0},{2,3},{3,2},{4,5},{5,4},{6,7},{7,6},{8,9},{9,8},{10,11... | collective-permute-start | bytes 196616 | tf_op jit(solution)/shard_map/ppermute | solution.py:131
  92.4 4.4 %collective-permute-start.16 = (f32[129,128]{1,0:T(8,128)S(1)}, f32[129,128]{1,0:T(8,128)S(1)}, u32[]{:S(2)}, u32[]{:S(2)}) collective-permute-start(f32[129,128]{1,0:T(8,128)S(1)} %add.98), channel_id=1, source_target_pairs={{0,1},{1,0},{2,3},{3,2},{4,5},{5,4},{6,7},{7,6},{8,9},{9,8},{10,11... | collective-permute-start | bytes 198152 | tf_op jit(solution)/shard_map/ppermute | solution.py:131
  92.6 6.0 %collective-permute-start.9 = (f32[128,128]{1,0:T(8,128)S(1)}, f32[128,128]{1,0:T(8,128)S(1)}, u32[]{:S(2)}, u32[]{:S(2)}) collective-permute-start(f32[128,128]{1,0:T(8,128)S(1)} %add.90), channel_id=1, source_target_pairs={{0,2},{1,3},{2,0},{3,1},{4,6},{5,7},{6,4},{7,5},{8,10},{9,11},{10,... | collective-permute-start | bytes 196616 | tf_op jit(solution)/shard_map/ppermute | solution.py:131
  96.8 5.9 %collective-permute-start.17 = (f32[129,128]{1,0:T(8,128)S(1)}, f32[129,128]{1,0:T(8,128)S(1)}, u32[]{:S(2)}, u32[]{:S(2)}) collective-permute-start(f32[129,128]{1,0:T(8,128)S(1)} %add.99), channel_id=1, source_target_pairs={{0,2},{1,3},{2,0},{3,1},{4,6},{5,7},{6,4},{7,5},{8,10},{9,11},{10,... | collective-permute-start | bytes 198152 | tf_op jit(solution)/shard_map/ppermute | solution.py:131
  98.6 5.7 %collective-permute-start.10 = (f32[128,128]{1,0:T(8,128)S(1)}, f32[128,128]{1,0:T(8,128)S(1)}, u32[]{:S(2)}, u32[]{:S(2)}) collective-permute-start(f32[128,128]{1,0:T(8,128)S(1)} %add.91), channel_id=1, source_target_pairs={{0,4},{1,5},{2,6},{3,7},{4,0},{5,1},{6,2},{7,3},{8,12},{9,13},{10,... | collective-permute-start | bytes 196616 | tf_op jit(solution)/shard_map/ppermute | solution.py:131
  102.8 4.4 %collective-permute-start.18 = (f32[129,128]{1,0:T(8,128)S(1)}, f32[129,128]{1,0:T(8,128)S(1)}, u32[]{:S(2)}, u32[]{:S(2)}) collective-permute-start(f32[129,128]{1,0:T(8,128)S(1)} %add.100), channel_id=1, source_target_pairs={{0,4},{1,5},{2,6},{3,7},{4,0},{5,1},{6,2},{7,3},{8,12},{9,13},{10,... | collective-permute-start | bytes 198152 | tf_op jit(solution)/shard_map/ppermute | solution.py:131
  104.4 6.1 %collective-permute-start.11 = (f32[128,128]{1,0:T(8,128)S(1)}, f32[128,128]{1,0:T(8,128)S(1)}, u32[]{:S(2)}, u32[]{:S(2)}) collective-permute-start(f32[128,128]{1,0:T(8,128)S(1)} %add.92), channel_id=1, source_target_pairs={{0,8},{1,9},{2,10},{3,11},{4,12},{5,13},{6,14},{7,15},{8,0},{9,1},... | collective-permute-start | bytes 196616 | tf_op jit(solution)/shard_map/ppermute | solution.py:131
  107.2 26.8 %collective-permute-start.19 = (f32[129,128]{1,0:T(8,128)S(1)}, f32[129,128]{1,0:T(8,128)S(1)}, u32[]{:S(2)}, u32[]{:S(2)}) collective-permute-start(f32[129,128]{1,0:T(8,128)S(1)} %add.101), channel_id=1, source_target_pairs={{0,8},{1,9},{2,10},{3,11},{4,12},{5,13},{6,14},{7,15},{8,0},{9,1},... | collective-permute-start | bytes 198152 | tf_op jit(solution)/shard_map/ppermute | solution.py:131
